TPU v7x, 512 devices: a whole 4x8x8 slice. The times are simulated.
512 devices in a mesh: dp: 8 (over y_hi, x), expert: 64 (over y_lo, z, core).
Axes of the slice: x: 4, y: 8 (y_hi: 2, y_lo: 4; y = y_hi * 4 + y_lo), z: 8, core: 2. Of those that a mesh axis runs over, the one named last changes fastest.
Arguments:
- tokens: bfloat16 [8192, 2560], P(('dp', 'expert')), may hold values from -6 to 6
- grad_out: bfloat16 [8192, 2560], P(('dp', 'expert')), may hold values from -6 to 6
- expert_ids: int32 [8192, 2], P(('dp', 'expert')), may hold values from 0 to 63, as said below
- gates: bfloat16 [8192, 2], P(('dp', 'expert')), may hold values from 0.099609375 to 1
- w_gate: bfloat16 [64, 2560, 1024], P('expert', None, 'dp'), may hold values from -0.125 to 0.125
- w_up: bfloat16 [64, 2560, 1024], P('expert', None, 'dp'), may hold values from -0.125 to 0.125
- w_down: bfloat16 [64, 1024, 2560], P('expert', 'dp'), may hold values from -0.1875 to 0.1875
Outputs:
- out_tokens: bfloat16 [8192, 2560], P(('dp', 'expert'))
- grad_tokens: bfloat16 [8192, 2560], P(('dp', 'expert'))
- grad_gate: bfloat16 [64, 2560, 1024], P('expert', None, 'dp')
- grad_up: bfloat16 [64, 2560, 1024], P('expert', None, 'dp')
- grad_down: bfloat16 [64, 1024, 2560], P('expert', 'dp')
Inputs may be any that keep to these rules, and one draw needn't show every extreme that they name: `expert_ids`: each token names 2 different experts. Over the tokens of all devices at one index of expert taken together, one expert, the same at every index, is named exactly 8 times; a second one, also the same at every index, exactly 5 times; every other expert at most 5 times.
All inputs are finite; a program needn't handle non-finite values.
Results may differ from a plain program's by a relative error of at most 0.019.
Values may be sent and summed in bfloat16 or wider, within the bound.
No kernel may reach another device: no remote copies, remote signals or barrier semaphores. Data moves between devices by JAX's collectives and lax.ppermute only.
A program may use at most 128 MiB of HBM per device.

v0:
```python
import jax
import jax.numpy as jnp
from jax import lax
from jax.sharding import PartitionSpec as P


def expert_rows(rows_in, cot_in, gate_weight, up_weight, down_weight):
    gate_pre = jnp.dot(rows_in, gate_weight, preferred_element_type=jnp.float32)
    up_pre = jnp.dot(rows_in, up_weight, preferred_element_type=jnp.float32)
    hidden = (jax.nn.silu(gate_pre) * up_pre).astype(jnp.bfloat16)
    partial_value = jnp.dot(hidden, down_weight, preferred_element_type=jnp.float32).astype(
        jnp.bfloat16
    )
    first_dim = (((0,), (0,)), ((), ()))
    last_dim = (((1,), (1,)), ((), ()))
    grad_down = lax.dot_general(hidden, cot_in, first_dim, preferred_element_type=jnp.float32)
    d_hidden = lax.dot_general(cot_in, down_weight, last_dim, preferred_element_type=jnp.float32)
    sig = jax.nn.sigmoid(gate_pre)
    d_gate = (d_hidden * up_pre * sig * (1.0 + gate_pre * (1.0 - sig))).astype(jnp.bfloat16)
    d_up = (d_hidden * gate_pre * sig).astype(jnp.bfloat16)
    grad_gate = lax.dot_general(rows_in, d_gate, first_dim, preferred_element_type=jnp.float32)
    grad_up = lax.dot_general(rows_in, d_up, first_dim, preferred_element_type=jnp.float32)
    back_term = lax.dot_general(d_gate, gate_weight, last_dim, preferred_element_type=jnp.float32)
    back_term = (
        back_term + lax.dot_general(d_up, up_weight, last_dim, preferred_element_type=jnp.float32)
    ).astype(jnp.bfloat16)
    return (partial_value, back_term, grad_gate, grad_up, grad_down)


def fill_slots(slot_index, slot_total, assigned, top_count, group_tokens, cot_rows):
    owner = jnp.full((slot_total,), assigned, jnp.int32)
    owner = owner.at[slot_index].set(jnp.arange(assigned, dtype=jnp.int32), mode="drop")
    filled = owner < assigned
    safe = jnp.where(filled, owner, 0)
    token_rows = jnp.take(group_tokens, safe // top_count, axis=0)
    cot_taken = jnp.take(cot_rows, safe, axis=0)
    token_rows = jnp.where(filled[:, None], token_rows, jnp.zeros((), token_rows.dtype))
    cot_taken = jnp.where(filled[:, None], cot_taken, jnp.zeros((), cot_taken.dtype))
    return (token_rows, cot_taken)


def collect_slots(values, slot_index, weights):
    taken = jnp.take(values, slot_index.reshape(-1), axis=0, mode="fill", fill_value=0)
    taken = taken.reshape(slot_index.shape[0], slot_index.shape[1], values.shape[1]).astype(
        jnp.float32
    )
    if weights is None:
        return jnp.sum(taken, axis=1)
    return jnp.sum(weights.astype(jnp.float32)[:, :, None] * taken, axis=1)


def body(tokens, grad_out, expert_ids, gates, w_gate, w_up, w_down):
    dp_count = lax.axis_size("dp")
    experts = lax.axis_size("expert")
    local_rows = tokens.shape[0]
    feature_width = tokens.shape[1]
    top_count = expert_ids.shape[1]
    group_rows = dp_count * local_rows
    assigned = group_rows * top_count
    mean_slots = assigned // experts
    cap_hot = 2 * mean_slots
    group_tokens, group_grads, group_ids, group_gates = (
        lax.all_gather(tokens, "dp", axis=0, tiled=True),
        lax.all_gather(grad_out, "dp", axis=0, tiled=True),
        lax.all_gather(expert_ids, "dp", axis=0, tiled=True),
        lax.all_gather(gates, "dp", axis=0, tiled=True),
    )
    flat_ids = group_ids.reshape(-1)
    expert_range = jnp.arange(experts, dtype=jnp.int32)
    member = (flat_ids[:, None] == expert_range[None, :]).astype(jnp.int32)
    before = jnp.sum((jnp.cumsum(member, axis=0) - member) * member, axis=1)
    cot_rows = (
        (group_gates.astype(jnp.float32)[:, :, None] * group_grads.astype(jnp.float32)[:, None, :])
        .astype(jnp.bfloat16)
        .reshape(assigned, feature_width)
    )
    goes_out = jnp.ones(flat_ids.shape, dtype=bool)
    slot_count = experts * cap_hot
    slot_of = jnp.where(goes_out, flat_ids * cap_hot + before, slot_count).astype(jnp.int32)
    send_rows, send_cot = fill_slots(
        slot_of, slot_count, assigned, top_count, group_tokens, cot_rows
    )
    arrived_rows, arrived_cot = (
        lax.all_to_all(
            send_rows.reshape(experts, cap_hot, feature_width),
            "expert",
            split_axis=0,
            concat_axis=0,
            tiled=True,
        ),
        lax.all_to_all(
            send_cot.reshape(experts, cap_hot, feature_width),
            "expert",
            split_axis=0,
            concat_axis=0,
            tiled=True,
        ),
    )
    partial_value, back_term, grad_gate, grad_up, grad_down = expert_rows(
        arrived_rows.reshape(slot_count, feature_width),
        arrived_cot.reshape(slot_count, feature_width),
        w_gate[0],
        w_up[0],
        w_down[0],
    )
    return_partial, return_back = (
        lax.all_to_all(
            partial_value.reshape(experts, cap_hot, feature_width),
            "expert",
            split_axis=0,
            concat_axis=0,
            tiled=True,
        ),
        lax.all_to_all(
            back_term.reshape(experts, cap_hot, feature_width),
            "expert",
            split_axis=0,
            concat_axis=0,
            tiled=True,
        ),
    )
    slot_pairs = slot_of.reshape(group_rows, top_count)
    out_part = collect_slots(
        return_partial.reshape(slot_count, feature_width), slot_pairs, group_gates
    )
    back_part = collect_slots(return_back.reshape(slot_count, feature_width), slot_pairs, None)
    out_sum, back_sum = (
        lax.psum_scatter(
            out_part.astype(jnp.bfloat16), "dp", scatter_dimension=0, tiled=True
        ).astype(jnp.float32),
        lax.psum_scatter(
            back_part.astype(jnp.bfloat16), "dp", scatter_dimension=0, tiled=True
        ).astype(jnp.float32),
    )
    return (
        out_sum.astype(jnp.bfloat16),
        back_sum.astype(jnp.bfloat16),
        grad_gate.astype(jnp.bfloat16)[None],
        grad_up.astype(jnp.bfloat16)[None],
        grad_down.astype(jnp.bfloat16)[None],
    )


def solution(mesh):
    in_specs = (
        P(("dp", "expert"), None),
        P(("dp", "expert"), None),
        P(("dp", "expert"), None),
        P(("dp", "expert"), None),
        P("expert", None, "dp"),
        P("expert", None, "dp"),
        P("expert", "dp", None),
    )
    out_specs = (
        P(("dp", "expert"), None),
        P(("dp", "expert"), None),
        P("expert", None, "dp"),
        P("expert", None, "dp"),
        P("expert", "dp", None),
    )
    return jax.shard_map(body, mesh=mesh, in_specs=in_specs, out_specs=out_specs, check_vma=False)
```

profile of v0, /device:TPU:56, one launch (start us, length us, event | category | flops | bytes accessed | tf_op | source)
XLA Modules:
  0.0 696.4 jit_solution(2245142333885996936)
XLA Ops:
  7.2 28.3 %all-gather.1 = s32[8,16,2]{1,2,0:T(2,128)S(1)} all-gather(s32[1,16,2]{1,2,0:T(2,128)} %bitcast.86), channel_id=1, replica_groups=mesh['dp'=8,'expert'=64] {'dp'}, dimensions={0}, use_global_device_ids=true | all-gather | bytes 1152 | tf_op jit(solution)/shard_map/all_gather | solution.py:65
  35.5 0.1 copy.28
  35.6 0.1 eq.25
  35.7 0.1 eq.29
  35.9 0.1 copy.32
  36.0 0.1 mul.77
  36.2 0.6 reduce-window.6
  36.8 0.2 slice_reduce_fusion
  37.1 1.4 scatter_custom_fusion
  38.6 23.2 %all-gather = bf16[8,16,2]{1,2,0:T(2,128)(2,1)S(1)} all-gather(bf16[1,16,2]{1,2,0:T(2,128)(2,1)} %bitcast.88), channel_id=1, replica_groups=mesh['dp'=8,'expert'=64] {'dp'}, dimensions={0}, use_global_device_ids=true | all-gather | bytes 576 | tf_op jit(solution)/shard_map/all_gather | solution.py:66
  61.7 0.1 copy.34
  61.9 0.1 mul.84
  62.2 0.3 copy-done.3
  62.6 45.8 %all_gather.14 = bf16[128,2560]{1,0:T(8,128)(2,1)S(1)} all-gather(bf16[16,2560]{1,0:T(8,128)(2,1)} %param.9), channel_id=1, replica_groups=mesh['dp'=8,'expert'=64] {'dp'}, dimensions={0}, use_global_device_ids=true | all-gather | bytes 737280 | tf_op jit(solution)/shard_map/all_gather | solution.py:63
  108.4 45.0 %all_gather.15 = bf16[128,2560]{1,0:T(8,128)(2,1)S(1)} all-gather(bf16[16,2560]{1,0:T(8,128)(2,1)} %param.10), channel_id=1, replica_groups=mesh['dp'=8,'expert'=64] {'dp'}, dimensions={0}, use_global_device_ids=true | all-gather | bytes 737280 | tf_op jit(solution)/shard_map/all_gather | solution.py:64
  153.4 2.2 mul.86
  155.6 4.5 mul.87
  160.1 3.5 gather_fusion
  163.6 1.9 multiply_convert_fusion
  165.6 3.5 gather_fusion.1
  169.0 4.0 fusion.8
  173.0 80.1 %all_to_all.20 = bf16[64,8,2560]{2,1,0:T(8,128)(2,1)S(1)} all-to-all(bf16[64,8,2560]{2,1,0:T(8,128)(2,1)S(1)} %get-tuple-element.14), channel_id=1, replica_groups=mesh['dp'=8,'expert'=64] {'expert'}, dimensions={0} | all-to-all | bytes 5242880 | tf_op jit(solution)/shard_map/all_to_all | solution.py:84
  253.1 8.6 %all-to-all-start.2 = ((bf16[64,8,2560]{2,1,0:T(8,128)(2,1)}), bf16[64,8,2560]{2,1,0:T(8,128)(2,1)}, u32[]{:S(2)}, u32[]{:S(2)}) async-start(bf16[64,8,2560]{2,1,0:T(8,128)(2,1)} %get-tuple-element.13), calls=%async_computation.3 | async-start | bytes 5242880 | tf_op jit(solution)/shard_map/all_to_all | solution.py:91
  261.7 2.0 fusion.11
  263.7 1.5 fusion.13
  265.3 64.1 %all-to-all-done.2 = bf16[64,8,2560]{2,1,0:T(8,128)(2,1)} async-done(((bf16[64,8,2560]{2,1,0:T(8,128)(2,1)}), bf16[64,8,2560]{2,1,0:T(8,128)(2,1)}, u32[]{:S(2)}, u32[]{:S(2)}) %all-to-all-start.2) | async-done | bytes 2621472 | tf_op jit(solution)/shard_map/all_to_all | solution.py:91
  329.4 3.3 multiply_convert_fusion.1
  332.7 0.6 copy-done.7
  333.3 2.3 fusion.1
  335.7 10.8 %all-to-all-start.1 = ((bf16[64,8,2560]{2,1,0:T(8,128)(2,1)}), bf16[64,8,2560]{2,1,0:T(8,128)(2,1)}, u32[]{:S(2)}, u32[]{:S(2)}) async-start(bf16[64,8,2560]{2,1,0:T(8,128)(2,1)} %fusion.1), calls=%async_computation.1 | async-start | bytes 5242880 | tf_op jit(solution)/shard_map/all_to_all | solution.py:107
  346.5 2.1 fusion.20
  348.6 2.4 fusion
  351.0 63.2 %all-to-all-done.1 = bf16[64,8,2560]{2,1,0:T(8,128)(2,1)} async-done(((bf16[64,8,2560]{2,1,0:T(8,128)(2,1)}), bf16[64,8,2560]{2,1,0:T(8,128)(2,1)}, u32[]{:S(2)}, u32[]{:S(2)}) %all-to-all-start.1) | async-done | bytes 2621472 | tf_op jit(solution)/shard_map/all_to_all | solution.py:107
  414.2 10.8 %all-to-all-start.3 = ((bf16[64,8,2560]{2,1,0:T(8,128)(2,1)}), bf16[64,8,2560]{2,1,0:T(8,128)(2,1)}, u32[]{:S(2)}, u32[]{:S(2)}) async-start(bf16[64,8,2560]{2,1,0:T(8,128)(2,1)} %fusion), calls=%async_computation.4 | async-start | bytes 5242880 | tf_op jit(solution)/shard_map/all_to_all | solution.py:114
  425.1 5.9 gather_fusion.2
  431.0 61.7 %all-to-all-done.3 = bf16[64,8,2560]{2,1,0:T(8,128)(2,1)} async-done(((bf16[64,8,2560]{2,1,0:T(8,128)(2,1)}), bf16[64,8,2560]{2,1,0:T(8,128)(2,1)}, u32[]{:S(2)}, u32[]{:S(2)}) %all-to-all-start.3) | async-done | bytes 2621472 | tf_op jit(solution)/shard_map/all_to_all | solution.py:114
  492.7 6.0 gather_fusion.3
  498.7 4.0 broadcast_select_fusion
  502.7 4.0 reshape.131
  506.7 5.4 reduce_sum.35
  512.1 0.3 reduce-scatter.3.cloned.1.call-start
  512.4 4.4 reshape.132
  516.8 6.3 multiply_reduce_fusion
  523.2 3.3 fusion.4
  526.4 1.7 fusion.3
  528.2 1.7 fusion.2
  529.9 67.5 %reduce-scatter.5.cloned.1.call-done = bf16[16,2560]{1,0:T(8,128)(2,1)} async-done(((bf16[128,2560]{1,0:T(8,128)(2,1)}), bf16[16,2560]{1,0:T(8,128)(2,1)}) %reduce-scatter.5.cloned.1.call-update) | async-done | bytes 81936 | tf_op jit(solution)/shard_map/reduce_scatter | solution.py:131
  597.4 92.1 %reduce-scatter.3.cloned.1.call-done = bf16[16,2560]{1,0:T(8,128)(2,1)} async-done(((bf16[128,2560]{1,0:T(8,128)(2,1)}), bf16[16,2560]{1,0:T(8,128)(2,1)}) %reduce-scatter.3.cloned.1.call-update) | async-done | bytes 81936 | tf_op jit(solution)/shard_map/reduce_scatter | solution.py:128
  (34 shorter events, 0.6 us)
Async XLA Ops:
  7.2 322.2 %copy-start = (bf16[1,128,2560]{2,1,0:T(8,128)(2,1)S(1)}, bf16[1,128,2560]{2,1,0:T(8,128)(2,1)}, u32[]{:S(2)}) copy-start(bf16[1,128,2560]{2,1,0:T(8,128)(2,1)} %param.15) | copy-start | bytes 1966084
  61.9 0.6 copy-start.3
  253.1 76.3 %all-to-all-start.2 = ((bf16[64,8,2560]{2,1,0:T(8,128)(2,1)}), bf16[64,8,2560]{2,1,0:T(8,128)(2,1)}, u32[]{:S(2)}, u32[]{:S(2)}) async-start(bf16[64,8,2560]{2,1,0:T(8,128)(2,1)} %get-tuple-element.13), calls=%async_computation.3 | async-start | bytes 5242880 | tf_op jit(solution)/shard_map/all_to_all | solution.py:91
  261.7 2.0 copy-start.2
  332.7 0.6 copy-start.7
  335.7 78.5 %all-to-all-start.1 = ((bf16[64,8,2560]{2,1,0:T(8,128)(2,1)}), bf16[64,8,2560]{2,1,0:T(8,128)(2,1)}, u32[]{:S(2)}, u32[]{:S(2)}) async-start(bf16[64,8,2560]{2,1,0:T(8,128)(2,1)} %fusion.1), calls=%async_computation.1 | async-start | bytes 5242880 | tf_op jit(solution)/shard_map/all_to_all | solution.py:107
  346.5 2.1 copy-start.1
  346.5 2.1 copy-start.5
  414.2 78.5 %all-to-all-start.3 = ((bf16[64,8,2560]{2,1,0:T(8,128)(2,1)}), bf16[64,8,2560]{2,1,0:T(8,128)(2,1)}, u32[]{:S(2)}, u32[]{:S(2)}) async-start(bf16[64,8,2560]{2,1,0:T(8,128)(2,1)} %fusion), calls=%async_computation.4 | async-start | bytes 5242880 | tf_op jit(solution)/shard_map/all_to_all | solution.py:114
  425.0 172.4 %reduce-scatter.5.cloned.1.call-start = ((), (), s32[]{:S(2)}) async-start(), calls=%async_computation.7 | async-start | bytes 737280 | tf_op jit(solution)/shard_map/reduce_scatter | solution.py:131
  512.1 177.4 %reduce-scatter.3.cloned.1.call-start = ((), (), s32[]{:S(2)}) async-start(), calls=%async_computation.6 | async-start | bytes 737280 | tf_op jit(solution)/shard_map/reduce_scatter | solution.py:128
  512.4 4.4 copy-start.4
  526.4 1.7 copy-start.6
Sparse Core Ops, SparseCore 0:
  512.2 85.1 reduce-scatter.4
  602.5 86.9 reduce-scatter.2
where the time goes:
time: 700 us; the launch traced here: 696 us
  waiting for transfers between devices  349 us (50%)
  blocking collectives  222 us (32%)
  local copies, waits for them, and re-layouts  37.7 us (5%)
  starting transfers between devices  30.5 us (4%)
  other arithmetic  22.5 us (3%)
  matrix products  20.4 us (3%)
  between operations  14.3 us (2%)
    reduce_scatter x1, waiting for transfers between devices, body(): lax.psum_scatter(out_part.astype(jnp.bfloat16), 'dp', scatter_dimension=0...  92.1 us
    all_to_all x1, blocking collectives, body(): lax.all_to_all(send_rows.reshape(experts, cap_hot, feature_width), 'exper...  80.1 us
    reduce_scatter x1, waiting for transfers between devices, body(): lax.psum_scatter(back_part.astype(jnp.bfloat16), 'dp', scatter_dimension=...  67.5 us
    all_to_all x1, waiting for transfers between devices, body(): lax.all_to_all(send_cot.reshape(experts, cap_hot, feature_width), 'expert...  64.1 us
    all_to_all x1, waiting for transfers between devices, body(): lax.all_to_all(partial_value.reshape(experts, cap_hot, feature_width), 'e...  63.2 us
    all_to_all x1, waiting for transfers between devices, body(): lax.all_to_all(back_term.reshape(experts, cap_hot, feature_width), 'exper...  61.7 us
    all_gather x1, blocking collectives, body(): lax.all_gather(tokens, 'dp', axis=0, tiled=True)  45.8 us
    all_gather x1, blocking collectives, body(): lax.all_gather(grad_out, 'dp', axis=0, tiled=True)  45 us
  transfers between devices with their start and end apart: 5, of which 5 were waited for; matrix products, arithmetic and copies ran while one was open for 5% of the time, Pallas kernels for 0%

commit v1 on v0

v1 whole, which is shorter than its diff:
```python
import jax
import jax.numpy as jnp
from jax import lax
from jax.sharding import PartitionSpec as P


def expert_rows(rows_in, cot_in, gate_weight, up_weight, down_weight):
    gate_pre = jnp.dot(rows_in, gate_weight, preferred_element_type=jnp.float32)
    up_pre = jnp.dot(rows_in, up_weight, preferred_element_type=jnp.float32)
    hidden = (jax.nn.silu(gate_pre) * up_pre).astype(jnp.bfloat16)
    partial_value = jnp.dot(hidden, down_weight, preferred_element_type=jnp.float32).astype(
        jnp.bfloat16
    )
    first_dim = (((0,), (0,)), ((), ()))
    last_dim = (((1,), (1,)), ((), ()))
    grad_down = lax.dot_general(hidden, cot_in, first_dim, preferred_element_type=jnp.float32)
    d_hidden = lax.dot_general(cot_in, down_weight, last_dim, preferred_element_type=jnp.float32)
    sig = jax.nn.sigmoid(gate_pre)
    d_gate = (d_hidden * up_pre * sig * (1.0 + gate_pre * (1.0 - sig))).astype(jnp.bfloat16)
    d_up = (d_hidden * gate_pre * sig).astype(jnp.bfloat16)
    grad_gate = lax.dot_general(rows_in, d_gate, first_dim, preferred_element_type=jnp.float32)
    grad_up = lax.dot_general(rows_in, d_up, first_dim, preferred_element_type=jnp.float32)
    back_term = lax.dot_general(d_gate, gate_weight, last_dim, preferred_element_type=jnp.float32)
    back_term = (
        back_term + lax.dot_general(d_up, up_weight, last_dim, preferred_element_type=jnp.float32)
    ).astype(jnp.bfloat16)
    return (partial_value, back_term, grad_gate, grad_up, grad_down)


def collect_slots(values, slot_index, weights):
    taken = jnp.take(values, slot_index.reshape(-1), axis=0, mode="fill", fill_value=0)
    taken = taken.reshape(slot_index.shape[0], slot_index.shape[1], values.shape[1]).astype(
        jnp.float32
    )
    if weights is None:
        return jnp.sum(taken, axis=1)
    return jnp.sum(weights.astype(jnp.float32)[:, :, None] * taken, axis=1)


def body(tokens, grad_out, expert_ids, gates, w_gate, w_up, w_down):
    dp_count = lax.axis_size("dp")
    experts = lax.axis_size("expert")
    local_rows = tokens.shape[0]
    width = tokens.shape[1]
    top_count = expert_ids.shape[1]
    group_rows = dp_count * local_rows
    assigned = group_rows * top_count
    mean_slots = assigned // experts
    cap_hot = 2 * mean_slots
    side = 128
    extra = jnp.concatenate(
        [
            expert_ids.astype(jnp.bfloat16),
            gates,
            jnp.zeros((local_rows, side - 2 * top_count), jnp.bfloat16),
        ],
        axis=1,
    )
    packed = jnp.concatenate([tokens, grad_out, extra], axis=1)
    group = lax.all_gather(packed, "dp", axis=0, tiled=True)
    group_tokens = group[:, :width]
    group_grads = group[:, width : 2 * width]
    group_ids = group[:, 2 * width : 2 * width + top_count].astype(jnp.int32)
    group_gates = group[:, 2 * width + top_count : 2 * width + 2 * top_count]

    flat_ids = group_ids.reshape(-1)
    expert_range = jnp.arange(experts, dtype=jnp.int32)
    member = (flat_ids[:, None] == expert_range[None, :]).astype(jnp.int32)
    before = jnp.sum((jnp.cumsum(member, axis=0) - member) * member, axis=1)
    slot_count = experts * cap_hot
    slot_of = (flat_ids * cap_hot + before).astype(jnp.int32)

    owner = jnp.full((slot_count,), assigned, jnp.int32)
    owner = owner.at[slot_of].set(jnp.arange(assigned, dtype=jnp.int32), mode="drop")
    filled = owner < assigned
    safe = jnp.where(filled, owner, 0)
    tok = safe // top_count
    gate_of = jnp.where(filled, group_gates.reshape(-1)[safe].astype(jnp.float32), 0.0)
    rows_taken = jnp.where(filled[:, None], group_tokens[tok], jnp.zeros((), jnp.bfloat16))
    cot_taken = (gate_of[:, None] * group_grads[tok].astype(jnp.float32)).astype(jnp.bfloat16)
    send = jnp.concatenate([rows_taken, cot_taken], axis=1)
    arrived = lax.all_to_all(
        send.reshape(experts, cap_hot, 2 * width), "expert", 0, 0, tiled=True
    ).reshape(slot_count, 2 * width)

    partial_value, back_term, grad_gate, grad_up, grad_down = expert_rows(
        arrived[:, :width],
        arrived[:, width:],
        w_gate[0],
        w_up[0],
        w_down[0],
    )
    ret = jnp.concatenate([partial_value, back_term], axis=1)
    returned = lax.all_to_all(
        ret.reshape(experts, cap_hot, 2 * width), "expert", 0, 0, tiled=True
    ).reshape(slot_count, 2 * width)
    slot_pairs = slot_of.reshape(group_rows, top_count)
    out_part = collect_slots(returned[:, :width], slot_pairs, group_gates)
    back_part = collect_slots(returned[:, width:], slot_pairs, None)
    both = jnp.concatenate([out_part, back_part], axis=1).astype(jnp.bfloat16)
    spread = lax.all_to_all(
        both.reshape(dp_count, local_rows, 2 * width), "dp", 0, 0, tiled=True
    )
    total = jnp.sum(spread.astype(jnp.float32), axis=0).astype(jnp.bfloat16)
    return (
        total[:, :width],
        total[:, width:],
        grad_gate.astype(jnp.bfloat16)[None],
        grad_up.astype(jnp.bfloat16)[None],
        grad_down.astype(jnp.bfloat16)[None],
    )


def solution(mesh):
    in_specs = (
        P(("dp", "expert"), None),
        P(("dp", "expert"), None),
        P(("dp", "expert"), None),
        P(("dp", "expert"), None),
        P("expert", None, "dp"),
        P("expert", None, "dp"),
        P("expert", "dp", None),
    )
    out_specs = (
        P(("dp", "expert"), None),
        P(("dp", "expert"), None),
        P("expert", None, "dp"),
        P("expert", None, "dp"),
        P("expert", "dp", None),
    )
    return jax.shard_map(body, mesh=mesh, in_specs=in_specs, out_specs=out_specs, check_vma=False)
```

time: 700 us -> 496 us (0.71)
  waiting for transfers between devices: 349 us -> 237 us
  blocking collectives: 222 us -> 145 us
    reduce_scatter x2 -> x0, waiting for transfers between devices: 160 us -> none  [the longest x1 92.1 us: body(): lax.psum_scatter(out_part.astype(jnp.bfloat16), 'dp', scatter_dimension=0...]
    all_gather x4 -> x0, blocking collectives: 142 us -> none  [the longest x1 45.8 us: body(): lax.all_gather(tokens, 'dp', axis=0, tiled=True)]
    all_gather x0 -> x1, waiting for transfers between devices: none -> 70.9 us  [body(): group = lax.all_gather(packed, 'dp', axis=0, tiled=True)]
    all_to_all x1, blocking collectives: 80.1 us -> 145 us  [body(): lax.all_to_all(send.reshape(experts, cap_hot, 2 * width), 'expert', 0, 0,...]
    all_to_all x3 -> x2, waiting for transfers between devices: 189 us -> 167 us  [the longest x1 147 us: body(): lax.all_to_all(ret.reshape(experts, cap_hot, 2 * width), 'expert', 0, 0,...]
    select_n x4 -> x5, other arithmetic: 8.01 us -> 0.27 us  [the longest x1 0.24 us: body(): jnp.where(filled[:, None], group_tokens[tok], jnp.zeros((), jnp.bfloat16))]
    all_to_all x3 -> x2, starting transfers between devices: 30.2 us -> 24.1 us  [the longest x1 14.9 us: body(): lax.all_to_all(ret.reshape(experts, cap_hot, 2 * width), 'expert', 0, 0,...]
  transfers between devices with their start and end apart: 5 -> 3, of which waited for: 5 -> 3; matrix products, arithmetic and copies ran while one was open for 5% -> 2% of each run, Pallas kernels for 0% -> 0%
where the time goes in v1:
time: 496 us; the launch traced here: 495 us
  waiting for transfers between devices  237 us (48%)
  blocking collectives  145 us (29%)
  local copies, waits for them, and re-layouts  36.9 us (7%)
  other arithmetic  24.2 us (5%)
  starting transfers between devices  24.1 us (5%)
  between operations  14.3 us (3%)
  matrix products  13.6 us (3%)
    all_to_all x1, waiting for transfers between devices, body(): lax.all_to_all(ret.reshape(experts, cap_hot, 2 * width), 'expert', 0, 0,...  147 us
    all_to_all x1, blocking collectives, body(): lax.all_to_all(send.reshape(experts, cap_hot, 2 * width), 'expert', 0, 0,...  145 us
    all_gather x1, waiting for transfers between devices, body(): group = lax.all_gather(packed, 'dp', axis=0, tiled=True)  70.9 us
    all_to_all x1, waiting for transfers between devices, body(): lax.all_to_all(both.reshape(dp_count, local_rows, 2 * width), 'dp', 0, 0,...  19.8 us
    all_to_all x1, starting transfers between devices, body(): lax.all_to_all(ret.reshape(experts, cap_hot, 2 * width), 'expert', 0, 0,...  14.9 us
  transfers between devices with their start and end apart: 3, of which 3 were waited for; matrix products, arithmetic and copies ran while one was open for 2% of the time, Pallas kernels for 0%

profile of v1, /device:TPU:56, one launch (start us, length us, event | category | flops | bytes accessed | tf_op | source)
XLA Modules:
  0.0 495.1 jit_solution(2697792149016737092)
XLA Ops:
  7.2 0.7 convert_element_type.70
  8.1 0.7 copy.18
  8.8 1.7 concatenate.19
  10.5 70.9 %all-gather.2.cloned.1.call-done = bf16[128,5248]{1,0:T(8,128)(2,1)} async-done(((bf16[16,5248]{1,0:T(8,128)(2,1)}), bf16[128,5248]{1,0:T(8,128)(2,1)}) %all-gather.2.cloned.1.call-update) | async-done | bytes 1343504 | tf_op jit(solution)/shard_map/all_gather | solution.py:60
  81.4 1.0 slice_convert_fusion.1
  82.4 0.1 eq.25
  82.5 0.1 eq.29
  82.7 0.8 broadcast_multiply_fusion
  83.5 0.1 mul.70
  83.6 0.6 reduce-window.6
  84.2 0.2 slice_reduce_fusion
  84.5 0.1 fusion.22
  84.6 1.4 scatter_custom_fusion
  86.1 0.1 reshape.105
  86.3 3.4 gather_fusion.1
  89.9 3.5 gather_fusion.2
  93.4 3.5 gather_fusion
  96.8 2.4 fusion
  99.2 0.1 copy-done.3
  99.4 0.2 bitcast_select_fusion
  99.6 0.8 pad_maximum_fusion
  100.4 144.5 %all_to_all.15 = bf16[64,8,5120]{2,1,0:T(8,128)(2,1)S(1)} all-to-all(bf16[64,8,5120]{2,1,0:T(8,128)(2,1)S(1)} %pad_maximum_fusion), channel_id=1, replica_groups=mesh['dp'=8,'expert'=64] {'expert'}, dimensions={0} | all-to-all | bytes 10485760 | tf_op jit(solution)/shard_map/all_to_all | solution.py:82
  244.9 0.8 fusion.5
  245.7 0.7 copy-done.6
  246.4 0.8 fusion.11
  247.3 0.9 multiply_convert_fusion.2
  248.2 0.8 convolution_convert_fusion
  249.0 0.8 fusion.17
  249.9 0.9 add_convert_fusion
  250.8 3.1 maximum_bitcast_fusion
  253.9 14.9 %all-to-all-start.1 = ((bf16[64,8,5120]{2,1,0:T(8,128)(2,1)}), bf16[64,8,5120]{2,1,0:T(8,128)(2,1)}, u32[]{:S(2)}, u32[]{:S(2)}) async-start(bf16[64,8,5120]{2,1,0:T(8,128)(2,1)} %maximum_bitcast_fusion), calls=%async_computation.1 | async-start | bytes 10485760 | tf_op jit(solution)/shard_map/all_to_all | solution.py:94
  268.8 146.7 %all-to-all-done.1 = bf16[64,8,5120]{2,1,0:T(8,128)(2,1)} async-done(((bf16[64,8,5120]{2,1,0:T(8,128)(2,1)}), bf16[64,8,5120]{2,1,0:T(8,128)(2,1)}, u32[]{:S(2)}, u32[]{:S(2)}) %all-to-all-start.1) | async-done | bytes 5242912 | tf_op jit(solution)/shard_map/all_to_all | solution.py:94
  415.6 4.4 fusion.28
  420.0 5.9 %gather_fusion.3 = bf16[256,2560]{1,0:T(8,128)(2,1)} fusion(bf16[512,2560]{1,0:T(8,128)(2,1)} %get-tuple-element.10, s32[1024]{0:T(1024)S(1)} %pad_clamp_fusion), kind=kCustom, calls=%fused_computation.clone | custom fusion | bytes 2622464 | tf_op jit(solution)/shard_map/jit(_take)/gather | solution.py:31
  425.9 2.5 gather_fusion.4
  428.4 3.9 select_convert_fusion
  432.3 3.2 reshape.110
  435.6 4.0 convert_element_type.86
  439.5 5.3 %reduce.1 = bf16[128,2560]{1,0:T(8,128)(2,1)} reduce(bf16[128,2,2560]{2,1,0:T(2,128)(2,1)} %convert_element_type.86, bf16[]{:T(256)} %constant.21.clone.1), dimensions={1}, to_apply=%region_5.7.clone | reduce | flops 327680 | bytes 1966082 | tf_op jit(solution)/shard_map/reduce_sum | solution.py:36
  444.9 3.7 multiply_reduce_fusion
  448.5 1.2 pad_maximum_fusion.1
  449.8 9.2 %all-to-all-start.2 = ((bf16[8,16,5120]{2,1,0:T(8,128)(2,1)}), bf16[8,16,5120]{2,1,0:T(8,128)(2,1)S(1)}, u32[]{:S(2)}, u32[]{:S(2)}) async-start(bf16[8,16,5120]{2,1,0:T(8,128)(2,1)} %pad_maximum_fusion.1), calls=%async_computation.2 | async-start | bytes 2621440 | tf_op jit(solution)/shard_map/all_to_all | solution.py:101
  458.9 3.3 fusion.3
  462.2 3.6 fusion.1
  465.8 1.7 fusion.2
  467.6 19.8 %all-to-all-done.2 = bf16[8,16,5120]{2,1,0:T(8,128)(2,1)S(1)} async-done(((bf16[8,16,5120]{2,1,0:T(8,128)(2,1)}), bf16[8,16,5120]{2,1,0:T(8,128)(2,1)S(1)}, u32[]{:S(2)}, u32[]{:S(2)}) %all-to-all-start.2) | async-done | bytes 1310752 | tf_op jit(solution)/shard_map/all_to_all | solution.py:101
  487.4 0.2 reduce_sum.45
  487.6 0.7 fusion.30
  (46 shorter events, 0.6 us)
Async XLA Ops:
  7.2 240.1 %copy-start = (bf16[1,2560,128]{2,1,0:T(8,128)(2,1)S(1)}, bf16[1,2560,128]{2,1,0:T(8,128)(2,1)}, u32[]{:S(2)}) copy-start(bf16[1,2560,128]{2,1,0:T(8,128)(2,1)} %param.14) | copy-start | bytes 1966084
  7.2 74.2 %all-gather.2.cloned.1.call-start = ((), (), s32[]{:S(2)}) async-start(), calls=%async_computation.3 | async-start | bytes 1511424 | tf_op jit(solution)/shard_map/all_gather | solution.py:60
  81.4 8.4 %copy-start.5 = (bf16[128,5248]{1,0:T(8,128)(2,1)S(1)}, bf16[128,5248]{1,0:T(8,128)(2,1)}, u32[]{:S(2)}) copy-start(bf16[128,5248]{1,0:T(8,128)(2,1)} %all-gather.2.cloned.1.call-done) | copy-start | bytes 4030468
  96.8 2.5 copy-start.3
  100.4 144.5 %copy-start.7 = (bf16[1,128,2560]{2,1,0:T(8,128)(2,1)S(1)}, bf16[1,128,2560]{2,1,0:T(8,128)(2,1)}, u32[]{:S(2)}) copy-start(bf16[1,128,2560]{2,1,0:T(8,128)(2,1)} %param.15) | copy-start | bytes 1966084
  244.9 2.4 copy-start.2
  244.9 1.5 copy-start.6
  248.2 1.7 copy-start.10
  248.2 1.7 copy-start.8
  253.9 161.7 %all-to-all-start.1 = ((bf16[64,8,5120]{2,1,0:T(8,128)(2,1)}), bf16[64,8,5120]{2,1,0:T(8,128)(2,1)}, u32[]{:S(2)}, u32[]{:S(2)}) async-start(bf16[64,8,5120]{2,1,0:T(8,128)(2,1)} %maximum_bitcast_fusion), calls=%async_computation.1 | async-start | bytes 10485760 | tf_op jit(solution)/shard_map/all_to_all | solution.py:94
  444.9 3.7 copy-start.4
  449.8 12.4 %copy-start.11 = (bf16[512,128]{1,0:T(8,128)(2,1)S(1)}, bf16[512,128]{1,0:T(8,128)(2,1)}, u32[]{:S(2)}) copy-start(bf16[512,128]{1,0:T(8,128)(2,1)} %copy-done.10) | copy-start | bytes 393220
  449.8 37.6 %all-to-all-start.2 = ((bf16[8,16,5120]{2,1,0:T(8,128)(2,1)}), bf16[8,16,5120]{2,1,0:T(8,128)(2,1)S(1)}, u32[]{:S(2)}, u32[]{:S(2)}) async-start(bf16[8,16,5120]{2,1,0:T(8,128)(2,1)} %pad_maximum_fusion.1), calls=%async_computation.2 | async-start | bytes 2621440 | tf_op jit(solution)/shard_map/all_to_all | solution.py:101
  458.9 6.8 %slice-start = ((s8[5242880]{0:T(1024)(128)(4,1)}), s8[4194304]{0:T(1024)(128)(4,1)S(1)}, s32[]{:S(2)}) async-start(s8[5242880]{0:T(1024)(128)(4,1)} %bitcast.67), calls=%async_computation.4 | async-start | bytes 8388608
  462.2 3.6 slice-start.1
  462.2 3.6 copy-start.9
  465.8 22.5 %copy-start.1 = (bf16[1,2560,128]{2,1,0:T(8,128)(2,1)S(1)}, bf16[1,2560,128]{2,1,0:T(8,128)(2,1)}, u32[]{:S(2)}) copy-start(bf16[1,2560,128]{2,1,0:T(8,128)(2,1)} %param.14) | copy-start | bytes 1966084
Sparse Core Ops, SparseCore 0:
  11.8 69.6 all-gather.1

commit v2 on v1

--- a/solution.py
+++ b/solution.py
@@ -27,16 +27,6 @@
     return (partial_value, back_term, grad_gate, grad_up, grad_down)
 
 
-def collect_slots(values, slot_index, weights):
-    taken = jnp.take(values, slot_index.reshape(-1), axis=0, mode="fill", fill_value=0)
-    taken = taken.reshape(slot_index.shape[0], slot_index.shape[1], values.shape[1]).astype(
-        jnp.float32
-    )
-    if weights is None:
-        return jnp.sum(taken, axis=1)
-    return jnp.sum(weights.astype(jnp.float32)[:, :, None] * taken, axis=1)
-
-
 def body(tokens, grad_out, expert_ids, gates, w_gate, w_up, w_down):
     dp_count = lax.axis_size("dp")
     experts = lax.axis_size("expert")
@@ -57,7 +47,8 @@
         axis=1,
     )
     packed = jnp.concatenate([tokens, grad_out, extra], axis=1)
-    group = lax.all_gather(packed, "dp", axis=0, tiled=True)
+    copies = jnp.broadcast_to(packed[None], (dp_count,) + packed.shape)
+    group = lax.all_to_all(copies, "dp", 0, 0, tiled=True).reshape(group_rows, packed.shape[1])
     group_tokens = group[:, :width]
     group_grads = group[:, width : 2 * width]
     group_ids = group[:, 2 * width : 2 * width + top_count].astype(jnp.int32)
@@ -68,16 +59,16 @@
     member = (flat_ids[:, None] == expert_range[None, :]).astype(jnp.int32)
     before = jnp.sum((jnp.cumsum(member, axis=0) - member) * member, axis=1)
     slot_count = experts * cap_hot
-    slot_of = (flat_ids * cap_hot + before).astype(jnp.int32)
-
-    owner = jnp.full((slot_count,), assigned, jnp.int32)
-    owner = owner.at[slot_of].set(jnp.arange(assigned, dtype=jnp.int32), mode="drop")
-    filled = owner < assigned
-    safe = jnp.where(filled, owner, 0)
-    tok = safe // top_count
-    gate_of = jnp.where(filled, group_gates.reshape(-1)[safe].astype(jnp.float32), 0.0)
-    rows_taken = jnp.where(filled[:, None], group_tokens[tok], jnp.zeros((), jnp.bfloat16))
-    cot_taken = (gate_of[:, None] * group_grads[tok].astype(jnp.float32)).astype(jnp.bfloat16)
+    slot_pairs = (flat_ids * cap_hot + before).astype(jnp.int32).reshape(group_rows, top_count)
+    slot_range = jnp.arange(slot_count, dtype=jnp.int32)[:, None]
+    pick = jnp.zeros((slot_count, group_rows), jnp.bfloat16)
+    weigh = jnp.zeros((slot_count, group_rows), jnp.bfloat16)
+    for k in range(top_count):
+        hit = slot_pairs[:, k][None, :] == slot_range
+        pick = jnp.where(hit, jnp.ones((), jnp.bfloat16), pick)
+        weigh = jnp.where(hit, group_gates[:, k][None, :], weigh)
+    rows_taken = jnp.dot(pick, group_tokens, preferred_element_type=jnp.float32).astype(jnp.bfloat16)
+    cot_taken = jnp.dot(weigh, group_grads, preferred_element_type=jnp.float32).astype(jnp.bfloat16)
     send = jnp.concatenate([rows_taken, cot_taken], axis=1)
     arrived = lax.all_to_all(
         send.reshape(experts, cap_hot, 2 * width), "expert", 0, 0, tiled=True
@@ -94,9 +85,13 @@
     returned = lax.all_to_all(
         ret.reshape(experts, cap_hot, 2 * width), "expert", 0, 0, tiled=True
     ).reshape(slot_count, 2 * width)
-    slot_pairs = slot_of.reshape(group_rows, top_count)
-    out_part = collect_slots(returned[:, :width], slot_pairs, group_gates)
-    back_part = collect_slots(returned[:, width:], slot_pairs, None)
+    first_dim = (((0,), (0,)), ((), ()))
+    out_part = lax.dot_general(
+        weigh, returned[:, :width], first_dim, preferred_element_type=jnp.float32
+    )
+    back_part = lax.dot_general(
+        pick, returned[:, width:], first_dim, preferred_element_type=jnp.float32
+    )
     both = jnp.concatenate([out_part, back_part], axis=1).astype(jnp.bfloat16)
     spread = lax.all_to_all(
         both.reshape(dp_count, local_rows, 2 * width), "dp", 0, 0, tiled=True

time: 496 us -> 393 us (0.79); the launches traced: 495 us -> 387 us
  waiting for transfers between devices: 237 us -> 20.9 us
  blocking collectives: 145 us -> 332 us
  local copies, waits for them, and re-layouts: 36.9 us -> 4.29 us
  other arithmetic: 24.2 us -> 4.49 us
  starting transfers between devices: 24.1 us -> 7.75 us
  between operations: 14.3 us -> 0.8 us
    all_to_all x0 -> x2, blocking collectives: none -> 173 us  [the longest x1 145 us: body(): lax.all_to_all(ret.reshape(experts, cap_hot, 2 * width), 'expert', 0, 0,...]
    all_to_all x1 -> x0, waiting for transfers between devices: 147 us -> none  [body(): lax.all_to_all(ret.reshape(experts, cap_hot, 2 * width), 'expert', 0, 0,...]
    all_gather x1 -> x0, waiting for transfers between devices: 70.9 us -> none  [body(): group = lax.all_gather(packed, 'dp', axis=0, tiled=True)]
    gather x5 -> x0, local copies, waits for them, and re-layouts: 18.7 us -> none  [the longest x2 8.42 us: collect_slots(): jnp.take(values, slot_index.reshape(-1), axis=0, mode='fill', fill_value=0)]
    all_to_all x1 -> x0, starting transfers between devices: 14.9 us -> none  [body(): lax.all_to_all(ret.reshape(experts, cap_hot, 2 * width), 'expert', 0, 0,...]
    all_to_all x1, blocking collectives: 145 us -> 159 us  [body(): lax.all_to_all(send.reshape(experts, cap_hot, 2 * width), 'expert', 0, 0,...]
    reduce_sum x2 -> x0, other arithmetic: 9.01 us -> none  [the longest x1 5.34 us: collect_slots(): return jnp.sum(taken, axis=1)]
    convert_element_type x3 -> x1, other arithmetic: 7.28 us -> 0.01 us  [body(): group_ids = group[:, 2 * width:2 * width + top_count].astype(jnp.int32)]
  transfers between devices with their start and end apart: 3 -> 1, of which waited for: 3 -> 1; matrix products, arithmetic and copies ran while one was open for 2% -> 2% of each run, Pallas kernels for 0% -> 0%
where the time goes in v2:
time: 393 us; the launch traced here: 387 us
  blocking collectives  332 us (84%)
  waiting for transfers between devices  20.9 us (5%)
  matrix products  16.4 us (4%)
  starting transfers between devices  7.75 us (2%)
  other arithmetic  4.49 us (1%)
  local copies, waits for them, and re-layouts  4.29 us (1%)
    all_to_all x1, blocking collectives, body(): lax.all_to_all(send.reshape(experts, cap_hot, 2 * width), 'expert', 0, 0,...  159 us
    all_to_all x1, blocking collectives, body(): lax.all_to_all(ret.reshape(experts, cap_hot, 2 * width), 'expert', 0, 0,...  145 us
    all_to_all x1, blocking collectives, body(): lax.all_to_all(copies, 'dp', 0, 0, tiled=True)  28 us
    all_to_all x1, waiting for transfers between devices, body(): lax.all_to_all(both.reshape(dp_count, local_rows, 2 * width), 'dp', 0, 0,...  20.9 us
  transfers between devices with their start and end apart: 1, of which 1 were waited for; matrix products, arithmetic and copies ran while one was open for 2% of the time, Pallas kernels for 0%

profile of v2, /device:TPU:56, one launch (start us, length us, event | category | flops | bytes accessed | tf_op | source)
XLA Modules:
  0.0 386.8 jit_solution(12857249336721821718)
XLA Ops:
  0.6 0.0 copy-start
  0.6 0.7 convert_element_type.47
  1.4 0.1 copy.18
  1.5 0.7 copy.19
  2.2 1.0 concatenate.18
  3.3 0.1 broadcast_in_dim.43
  3.4 28.0 %all_to_all.20 = bf16[8,16,5248]{2,1,0:T(8,128)(2,1)S(1)} all-to-all(bf16[8,16,5248]{2,1,0:T(8,128)(2,1)S(1)} %broadcast_in_dim.43), channel_id=1, replica_groups=mesh['dp'=8,'expert'=64] {'dp'}, dimensions={0} | all-to-all | bytes 2686976 | tf_op jit(solution)/shard_map/all_to_all | solution.py:51
  31.3 0.2 slice_reduce_fusion.4
  31.6 0.1 eq.55
  31.7 0.1 eq.59
  31.8 0.6 reduce-window.6
  32.5 0.2 slice_reduce_fusion.2
  32.7 0.1 fusion.41
  32.8 0.1 reduce_sum.24
  33.0 0.2 slice_reduce_fusion.1
  33.1 0.8 convolution_convert_fusion.2
  34.0 0.8 convolution_convert_fusion.1
  34.8 0.8 maximum_bitcast_fusion
  35.6 0.0 copy-start.3
  35.6 158.7 %all_to_all.21 = bf16[64,8,5120]{2,1,0:T(8,128)(2,1)S(1)} all-to-all(bf16[64,8,5120]{2,1,0:T(8,128)(2,1)S(1)} %maximum_bitcast_fusion), channel_id=1, replica_groups=mesh['dp'=8,'expert'=64] {'expert'}, dimensions={0} | all-to-all | bytes 10485760 | tf_op jit(solution)/shard_map/all_to_all | solution.py:73
  194.3 0.0 copy-start.1
  194.3 0.0 copy-start.2
  194.3 0.0 copy-done.3
  194.3 0.9 fusion.6
  195.2 0.7 copy-done.2
  195.9 0.8 fusion.12
  196.7 0.0 copy-done.1
  196.7 0.0 copy-done
  196.7 0.9 multiply_convert_fusion.2
  197.6 0.8 convolution_convert_fusion
  198.4 0.8 fusion.20
  199.3 0.9 add_convert_fusion
  200.1 0.8 maximum_bitcast_fusion.1
  200.9 145.4 %all_to_all.22 = bf16[64,8,5120]{2,1,0:T(8,128)(2,1)S(1)} all-to-all(bf16[64,8,5120]{2,1,0:T(8,128)(2,1)S(1)} %maximum_bitcast_fusion.1), channel_id=1, replica_groups=mesh['dp'=8,'expert'=64] {'expert'}, dimensions={0} | all-to-all | bytes 10485760 | tf_op jit(solution)/shard_map/all_to_all | solution.py:85
  346.3 0.6 convolution_convert_fusion.7
  346.9 0.6 convolution_convert_fusion.6
  347.5 1.2 pad_maximum_fusion
  348.7 7.8 %all-to-all-start.3 = ((bf16[8,16,5120]{2,1,0:T(8,128)(2,1)}), bf16[8,16,5120]{2,1,0:T(8,128)(2,1)S(1)}, u32[]{:S(2)}, u32[]{:S(2)}) async-start(bf16[8,16,5120]{2,1,0:T(8,128)(2,1)} %pad_maximum_fusion), calls=%async_computation.3 | async-start | bytes 2621440 | tf_op jit(solution)/shard_map/all_to_all | solution.py:96
  356.4 0.0 slice-start
  356.4 3.3 fusion.2
  359.7 0.0 slice-start.1
  359.7 3.6 fusion
  363.3 0.0 slice-done
  363.3 0.0 slice-done.1
  363.3 1.7 fusion.1
  365.0 20.9 %all-to-all-done.3 = bf16[8,16,5120]{2,1,0:T(8,128)(2,1)S(1)} async-done(((bf16[8,16,5120]{2,1,0:T(8,128)(2,1)}), bf16[8,16,5120]{2,1,0:T(8,128)(2,1)S(1)}, u32[]{:S(2)}, u32[]{:S(2)}) %all-to-all-start.3) | async-done | bytes 1310752 | tf_op jit(solution)/shard_map/all_to_all | solution.py:96
  385.9 0.2 reduce_sum.25
  386.1 0.7 fusion.59
  (7 shorter events, 0.1 us)
Async XLA Ops:
  0.6 196.1 %copy-start = (bf16[1,2560,128]{2,1,0:T(8,128)(2,1)S(1)}, bf16[1,2560,128]{2,1,0:T(8,128)(2,1)}, u32[]{:S(2)}) copy-start(bf16[1,2560,128]{2,1,0:T(8,128)(2,1)} %param.12) | copy-start | bytes 1966084
  35.6 158.7 %copy-start.3 = (bf16[1,128,2560]{2,1,0:T(8,128)(2,1)S(1)}, bf16[1,128,2560]{2,1,0:T(8,128)(2,1)}, u32[]{:S(2)}) copy-start(bf16[1,128,2560]{2,1,0:T(8,128)(2,1)} %param.13) | copy-start | bytes 1966084
  194.3 2.4 copy-start.1
  194.3 1.5 copy-start.2
  348.7 37.2 %all-to-all-start.3 = ((bf16[8,16,5120]{2,1,0:T(8,128)(2,1)}), bf16[8,16,5120]{2,1,0:T(8,128)(2,1)S(1)}, u32[]{:S(2)}, u32[]{:S(2)}) async-start(bf16[8,16,5120]{2,1,0:T(8,128)(2,1)} %pad_maximum_fusion), calls=%async_computation.3 | async-start | bytes 2621440 | tf_op jit(solution)/shard_map/all_to_all | solution.py:96
  356.4 6.8 %slice-start = ((s8[5242880]{0:T(1024)(128)(4,1)}), s8[4194304]{0:T(1024)(128)(4,1)S(1)}, s32[]{:S(2)}) async-start(s8[5242880]{0:T(1024)(128)(4,1)} %bitcast.62), calls=%async_computation.4 | async-start | bytes 8388608
  359.7 3.6 slice-start.1

commit v3 on v2

v3 whole, which is shorter than its diff:
```python
import jax
import jax.numpy as jnp
from jax import lax
from jax.sharding import PartitionSpec as P


def dp_gather(block, dp_count):
    copies = jnp.broadcast_to(block[None], (dp_count,) + block.shape)
    gathered = lax.all_to_all(copies, "dp", 0, 0, tiled=True)
    return gathered.reshape(dp_count * block.shape[0], block.shape[1])


def expert_swap(block, experts, cap):
    shaped = block.reshape(experts, cap, block.shape[1])
    return lax.all_to_all(shaped, "expert", 0, 0, tiled=True).reshape(block.shape)


def dp_sum(part, dp_count, local_rows):
    spread = lax.all_to_all(
        part.astype(jnp.bfloat16).reshape(dp_count, local_rows, part.shape[1]), "dp", 0, 0, tiled=True
    )
    return jnp.sum(spread.astype(jnp.float32), axis=0).astype(jnp.bfloat16)


def body(tokens, grad_out, expert_ids, gates, w_gate, w_up, w_down):
    dp_count = lax.axis_size("dp")
    experts = lax.axis_size("expert")
    local_rows = tokens.shape[0]
    width = tokens.shape[1]
    top_count = expert_ids.shape[1]
    group_rows = dp_count * local_rows
    assigned = group_rows * top_count
    mean_slots = assigned // experts
    cap_hot = 2 * mean_slots
    side = 128
    extra = jnp.concatenate(
        [
            expert_ids.astype(jnp.bfloat16),
            gates,
            jnp.zeros((local_rows, side - 2 * top_count), jnp.bfloat16),
        ],
        axis=1,
    )
    group = dp_gather(jnp.concatenate([tokens, extra], axis=1), dp_count)
    group_grads = dp_gather(grad_out, dp_count)
    group_tokens = group[:, :width]
    group_ids = group[:, width : width + top_count].astype(jnp.int32)
    group_gates = group[:, width + top_count : width + 2 * top_count]

    flat_ids = group_ids.reshape(-1)
    expert_range = jnp.arange(experts, dtype=jnp.int32)
    member = (flat_ids[:, None] == expert_range[None, :]).astype(jnp.int32)
    before = jnp.sum((jnp.cumsum(member, axis=0) - member) * member, axis=1)
    slot_count = experts * cap_hot
    slot_pairs = (flat_ids * cap_hot + before).astype(jnp.int32).reshape(group_rows, top_count)
    slot_range = jnp.arange(slot_count, dtype=jnp.int32)[:, None]
    pick = jnp.zeros((slot_count, group_rows), jnp.bfloat16)
    weigh = jnp.zeros((slot_count, group_rows), jnp.bfloat16)
    for k in range(top_count):
        hit = slot_pairs[:, k][None, :] == slot_range
        pick = jnp.where(hit, jnp.ones((), jnp.bfloat16), pick)
        weigh = jnp.where(hit, group_gates[:, k][None, :], weigh)
    first_dim = (((0,), (0,)), ((), ()))
    last_dim = (((1,), (1,)), ((), ()))

    rows_taken = jnp.dot(pick, group_tokens, preferred_element_type=jnp.float32).astype(jnp.bfloat16)
    rows_in = expert_swap(rows_taken, experts, cap_hot)
    gate_weight, up_weight, down_weight = w_gate[0], w_up[0], w_down[0]
    gate_pre = jnp.dot(rows_in, gate_weight, preferred_element_type=jnp.float32)
    up_pre = jnp.dot(rows_in, up_weight, preferred_element_type=jnp.float32)
    hidden = (jax.nn.silu(gate_pre) * up_pre).astype(jnp.bfloat16)
    partial_value = jnp.dot(hidden, down_weight, preferred_element_type=jnp.float32).astype(
        jnp.bfloat16
    )
    partial_back = expert_swap(partial_value, experts, cap_hot)
    out_part = lax.dot_general(weigh, partial_back, first_dim, preferred_element_type=jnp.float32)
    out_sum = dp_sum(out_part, dp_count, local_rows)

    cot_taken = jnp.dot(weigh, group_grads, preferred_element_type=jnp.float32).astype(jnp.bfloat16)
    cot_in = expert_swap(cot_taken, experts, cap_hot)
    d_hidden = lax.dot_general(cot_in, down_weight, last_dim, preferred_element_type=jnp.float32)
    sig = jax.nn.sigmoid(gate_pre)
    d_gate = (d_hidden * up_pre * sig * (1.0 + gate_pre * (1.0 - sig))).astype(jnp.bfloat16)
    d_up = (d_hidden * gate_pre * sig).astype(jnp.bfloat16)
    back_term = lax.dot_general(d_gate, gate_weight, last_dim, preferred_element_type=jnp.float32)
    back_term = (
        back_term + lax.dot_general(d_up, up_weight, last_dim, preferred_element_type=jnp.float32)
    ).astype(jnp.bfloat16)
    back_ret = expert_swap(back_term, experts, cap_hot)
    back_part = lax.dot_general(pick, back_ret, first_dim, preferred_element_type=jnp.float32)
    back_sum = dp_sum(back_part, dp_count, local_rows)

    grad_down = lax.dot_general(hidden, cot_in, first_dim, preferred_element_type=jnp.float32)
    grad_gate = lax.dot_general(rows_in, d_gate, first_dim, preferred_element_type=jnp.float32)
    grad_up = lax.dot_general(rows_in, d_up, first_dim, preferred_element_type=jnp.float32)
    return (
        out_sum,
        back_sum,
        grad_gate.astype(jnp.bfloat16)[None],
        grad_up.astype(jnp.bfloat16)[None],
        grad_down.astype(jnp.bfloat16)[None],
    )


def solution(mesh):
    in_specs = (
        P(("dp", "expert"), None),
        P(("dp", "expert"), None),
        P(("dp", "expert"), None),
        P(("dp", "expert"), None),
        P("expert", None, "dp"),
        P("expert", None, "dp"),
        P("expert", "dp", None),
    )
    out_specs = (
        P(("dp", "expert"), None),
        P(("dp", "expert"), None),
        P("expert", None, "dp"),
        P("expert", None, "dp"),
        P("expert", "dp", None),
    )
    return jax.shard_map(body, mesh=mesh, in_specs=in_specs, out_specs=out_specs, check_vma=False)
```

time: 393 us -> 428 us (1.089); the launches traced: 387 us -> 426 us
  blocking collectives: 332 us -> 20.2 us
  waiting for transfers between devices: 20.9 us -> 281 us
  starting transfers between devices: 7.75 us -> 80.3 us
  matrix products: 16.4 us -> 32.3 us
    all_to_all x3 -> x1, blocking collectives: 332 us -> 20.2 us  [dp_gather(): gathered = lax.all_to_all(copies, 'dp', 0, 0, tiled=True)]
    all_to_all x1 -> x7, waiting for transfers between devices: 20.9 us -> 281 us  [the longest x4 255 us: expert_swap(): lax.all_to_all(shaped, 'expert', 0, 0, tiled=True).reshape(block.shape)]
    all_to_all x1 -> x7, starting transfers between devices: 7.75 us -> 80.3 us  [the longest x4 48.9 us: expert_swap(): lax.all_to_all(shaped, 'expert', 0, 0, tiled=True).reshape(block.shape)]
    dot_general x11, matrix products: 14.8 us -> 26.5 us  [the longest x1 3.28 us: body(): lax.dot_general(cot_in, down_weight, last_dim, preferred_element_type=jnp...]
  transfers between devices with their start and end apart: 1 -> 7, of which waited for: 1 -> 7; matrix products, arithmetic and copies ran while one was open for 2% -> 7% of each run, Pallas kernels for 0% -> 0%
where the time goes in v3:
time: 428 us; the launch traced here: 426 us
  waiting for transfers between devices  281 us (66%)
  starting transfers between devices  80.3 us (19%)
  matrix products  32.3 us (8%)
  blocking collectives  20.2 us (5%)
  local copies, waits for them, and re-layouts  7.05 us (2%)
  other arithmetic  5.2 us (1%)
    all_to_all x4, waiting for transfers between devices, expert_swap(): lax.all_to_all(shaped, 'expert', 0, 0, tiled=True).reshape(block.shape)  255 us
    all_to_all x4, starting transfers between devices, expert_swap(): lax.all_to_all(shaped, 'expert', 0, 0, tiled=True).reshape(block.shape)  48.9 us
    all_to_all x1, blocking collectives, dp_gather(): gathered = lax.all_to_all(copies, 'dp', 0, 0, tiled=True)  20.2 us
    all_to_all x2, starting transfers between devices, dp_sum(): lax.all_to_all(part.astype(jnp.bfloat16).reshape(dp_count, local_rows, pa...  17.9 us
    all_to_all x2, waiting for transfers between devices, dp_sum(): lax.all_to_all(part.astype(jnp.bfloat16).reshape(dp_count, local_rows, pa...  17.4 us
    all_to_all x1, starting transfers between devices, dp_gather(): gathered = lax.all_to_all(copies, 'dp', 0, 0, tiled=True)  13.5 us
  transfers between devices with their start and end apart: 7, of which 7 were waited for; matrix products, arithmetic and copies ran while one was open for 7% of the time, Pallas kernels for 0%

profile of v3, /device:TPU:56, one launch (start us, length us, event | category | flops | bytes accessed | tf_op | source)
XLA Modules:
  0.0 426.5 jit_solution(12550107777567284521)
XLA Ops:
  0.6 0.0 copy-start
  0.6 0.7 convert_element_type.53
  1.4 0.1 copy.18
  1.5 0.7 copy.19
  2.2 1.0 concatenate.3
  3.2 0.1 broadcast_in_dim.49
  3.3 20.2 %all_to_all.40 = bf16[8,16,2688]{2,1,0:T(8,128)(2,1)S(1)} all-to-all(bf16[8,16,2688]{2,1,0:T(8,128)(2,1)S(1)} %broadcast_in_dim.49), channel_id=1, replica_groups=mesh['dp'=8,'expert'=64] {'dp'}, dimensions={0} | all-to-all | bytes 1376256 | tf_op jit(solution)/shard_map/all_to_all | solution.py:9
  23.5 1.8 broadcast_in_dim.55
  25.3 13.5 %all-to-all-start.4 = ((bf16[8,16,2560]{2,1,0:T(8,128)(2,1)}), bf16[8,16,2560]{2,1,0:T(8,128)(2,1)S(1)}, u32[]{:S(2)}, u32[]{:S(2)}) async-start(bf16[8,16,2560]{2,1,0:T(8,128)(2,1)} %broadcast_in_dim.55), calls=%async_computation.4 | async-start | bytes 1310720 | tf_op jit(solution)/shard_map/all_to_all | solution.py:9
  38.8 0.1 eq.55
  39.0 0.1 eq.59
  39.1 0.6 reduce-window.6
  39.7 0.2 slice_reduce_fusion.2
  40.0 0.1 fusion.44
  40.1 0.1 reduce_sum.36
  40.3 0.2 slice_reduce_fusion.1
  40.4 2.3 fusion.1
  42.8 8.0 %all-to-all-done.4 = bf16[8,16,2560]{2,1,0:T(8,128)(2,1)S(1)} async-done(((bf16[8,16,2560]{2,1,0:T(8,128)(2,1)}), bf16[8,16,2560]{2,1,0:T(8,128)(2,1)S(1)}, u32[]{:S(2)}, u32[]{:S(2)}) %all-to-all-start.4) | async-done | bytes 655392 | tf_op jit(solution)/shard_map/all_to_all | solution.py:9
  50.8 0.8 copy-done.4
  51.6 16.5 %all-to-all-start.1 = ((bf16[64,8,2560]{2,1,0:T(8,128)(2,1)}), bf16[64,8,2560]{2,1,0:T(8,128)(2,1)S(1)}, u32[]{:S(2)}, u32[]{:S(2)}) async-start(bf16[64,8,2560]{2,1,0:T(8,128)(2,1)} %fusion.1), calls=%async_computation.1 | async-start | bytes 5242880 | tf_op jit(solution)/shard_map/all_to_all | solution.py:15
  68.1 1.0 slice_reduce_fusion.4
  69.1 3.5 fusion.3
  72.6 63.2 %all-to-all-done.1 = bf16[64,8,2560]{2,1,0:T(8,128)(2,1)S(1)} async-done(((bf16[64,8,2560]{2,1,0:T(8,128)(2,1)}), bf16[64,8,2560]{2,1,0:T(8,128)(2,1)S(1)}, u32[]{:S(2)}, u32[]{:S(2)}) %all-to-all-start.1) | async-done | bytes 2621472 | tf_op jit(solution)/shard_map/all_to_all | solution.py:15
  135.7 10.7 %all-to-all-start.5 = ((bf16[64,8,2560]{2,1,0:T(8,128)(2,1)}), bf16[64,8,2560]{2,1,0:T(8,128)(2,1)}, u32[]{:S(2)}, u32[]{:S(2)}) async-start(bf16[64,8,2560]{2,1,0:T(8,128)(2,1)} %fusion.3), calls=%async_computation.5 | async-start | bytes 5242880 | tf_op jit(solution)/shard_map/all_to_all | solution.py:15
  146.5 2.0 fusion.14
  148.5 1.5 fusion.16
  150.0 64.1 %all-to-all-done.5 = bf16[64,8,2560]{2,1,0:T(8,128)(2,1)} async-done(((bf16[64,8,2560]{2,1,0:T(8,128)(2,1)}), bf16[64,8,2560]{2,1,0:T(8,128)(2,1)}, u32[]{:S(2)}, u32[]{:S(2)}) %all-to-all-start.5) | async-done | bytes 2621472 | tf_op jit(solution)/shard_map/all_to_all | solution.py:15
  214.2 3.3 multiply_convert_fusion
  217.5 0.6 copy-done.7
  218.1 2.4 fusion.2
  220.5 10.9 %all-to-all-start.2 = ((bf16[64,8,2560]{2,1,0:T(8,128)(2,1)}), bf16[64,8,2560]{2,1,0:T(8,128)(2,1)}, u32[]{:S(2)}, u32[]{:S(2)}) async-start(bf16[64,8,2560]{2,1,0:T(8,128)(2,1)} %fusion.2), calls=%async_computation.2 | async-start | bytes 5242880 | tf_op jit(solution)/shard_map/all_to_all | solution.py:15
  231.4 0.0 copy-start.2
  231.5 2.0 fusion.23
  233.5 2.4 fusion
  235.9 63.2 %all-to-all-done.2 = bf16[64,8,2560]{2,1,0:T(8,128)(2,1)} async-done(((bf16[64,8,2560]{2,1,0:T(8,128)(2,1)}), bf16[64,8,2560]{2,1,0:T(8,128)(2,1)}, u32[]{:S(2)}, u32[]{:S(2)}) %all-to-all-start.2) | async-done | bytes 2621472 | tf_op jit(solution)/shard_map/all_to_all | solution.py:15
  299.1 10.8 %all-to-all-start.6 = ((bf16[64,8,2560]{2,1,0:T(8,128)(2,1)}), bf16[64,8,2560]{2,1,0:T(8,128)(2,1)}, u32[]{:S(2)}, u32[]{:S(2)}) async-start(bf16[64,8,2560]{2,1,0:T(8,128)(2,1)} %fusion), calls=%async_computation.6 | async-start | bytes 5242880 | tf_op jit(solution)/shard_map/all_to_all | solution.py:15
  309.9 3.1 convolution_convert_fusion.7
  313.1 64.6 %all-to-all-done.6 = bf16[64,8,2560]{2,1,0:T(8,128)(2,1)} async-done(((bf16[64,8,2560]{2,1,0:T(8,128)(2,1)}), bf16[64,8,2560]{2,1,0:T(8,128)(2,1)}, u32[]{:S(2)}, u32[]{:S(2)}) %all-to-all-start.6) | async-done | bytes 2621472 | tf_op jit(solution)/shard_map/all_to_all | solution.py:15
  377.7 8.9 %all-to-all-start.3 = ((bf16[8,16,2560]{2,1,0:T(8,128)(2,1)}), bf16[8,16,2560]{2,1,0:T(8,128)(2,1)}, u32[]{:S(2)}, u32[]{:S(2)}) async-start(bf16[8,16,2560]{2,1,0:T(8,128)(2,1)} %bitcast.89), calls=%async_computation.3 | async-start | bytes 1310720 | tf_op jit(solution)/shard_map/all_to_all | solution.py:19
  386.6 3.1 convolution_convert_fusion.6
  389.7 12.9 %all-to-all-done.3 = bf16[8,16,2560]{2,1,0:T(8,128)(2,1)} async-done(((bf16[8,16,2560]{2,1,0:T(8,128)(2,1)}), bf16[8,16,2560]{2,1,0:T(8,128)(2,1)}, u32[]{:S(2)}, u32[]{:S(2)}) %all-to-all-start.3) | async-done | bytes 655392 | tf_op jit(solution)/shard_map/all_to_all | solution.py:19
  402.6 9.0 %all-to-all-start.7 = ((bf16[8,16,2560]{2,1,0:T(8,128)(2,1)}), bf16[8,16,2560]{2,1,0:T(8,128)(2,1)}, u32[]{:S(2)}, u32[]{:S(2)}) async-start(bf16[8,16,2560]{2,1,0:T(8,128)(2,1)} %bitcast.88), calls=%async_computation.7 | async-start | bytes 1310720 | tf_op jit(solution)/shard_map/all_to_all | solution.py:19
  411.7 3.2 fusion.6
  414.8 1.7 fusion.5
  416.6 1.7 fusion.4
  418.3 1.8 reduce_sum.37
  420.1 4.5 %all-to-all-done.7 = bf16[8,16,2560]{2,1,0:T(8,128)(2,1)} async-done(((bf16[8,16,2560]{2,1,0:T(8,128)(2,1)}), bf16[8,16,2560]{2,1,0:T(8,128)(2,1)}, u32[]{:S(2)}, u32[]{:S(2)}) %all-to-all-start.7) | async-done | bytes 655392 | tf_op jit(solution)/shard_map/all_to_all | solution.py:19
  424.6 1.8 reduce_sum.38
  (18 shorter events, 0.1 us)
Async XLA Ops:
  0.6 213.5 %copy-start = (bf16[1,128,2560]{2,1,0:T(8,128)(2,1)S(1)}, bf16[1,128,2560]{2,1,0:T(8,128)(2,1)}, u32[]{:S(2)}) copy-start(bf16[1,128,2560]{2,1,0:T(8,128)(2,1)} %param.13) | copy-start | bytes 1966084
  23.5 19.3 %copy-start.1 = (bf16[8,16,2688]{2,1,0:T(8,128)(2,1)}, bf16[8,16,2688]{2,1,0:T(8,128)(2,1)S(1)}, u32[]{:S(2)}) copy-start(bf16[8,16,2688]{2,1,0:T(8,128)(2,1)S(1)} %all_to_all.40) | copy-start | bytes 2064388
  25.3 25.5 %all-to-all-start.4 = ((bf16[8,16,2560]{2,1,0:T(8,128)(2,1)}), bf16[8,16,2560]{2,1,0:T(8,128)(2,1)S(1)}, u32[]{:S(2)}, u32[]{:S(2)}) async-start(bf16[8,16,2560]{2,1,0:T(8,128)(2,1)} %broadcast_in_dim.55), calls=%async_computation.4 | async-start | bytes 1310720 | tf_op jit(solution)/shard_map/all_to_all | solution.py:9
  50.8 0.8 copy-start.4
  51.6 84.1 %all-to-all-start.1 = ((bf16[64,8,2560]{2,1,0:T(8,128)(2,1)}), bf16[64,8,2560]{2,1,0:T(8,128)(2,1)S(1)}, u32[]{:S(2)}, u32[]{:S(2)}) async-start(bf16[64,8,2560]{2,1,0:T(8,128)(2,1)} %fusion.1), calls=%async_computation.1 | async-start | bytes 5242880 | tf_op jit(solution)/shard_map/all_to_all | solution.py:15
  135.7 78.4 %all-to-all-start.5 = ((bf16[64,8,2560]{2,1,0:T(8,128)(2,1)}), bf16[64,8,2560]{2,1,0:T(8,128)(2,1)}, u32[]{:S(2)}, u32[]{:S(2)}) async-start(bf16[64,8,2560]{2,1,0:T(8,128)(2,1)} %fusion.3), calls=%async_computation.5 | async-start | bytes 5242880 | tf_op jit(solution)/shard_map/all_to_all | solution.py:15
  146.5 2.0 copy-start.3
  217.5 0.6 copy-start.7
  220.5 11.0 %copy-start.6 = (bf16[512,128]{1,0:T(8,128)(2,1)S(1)}, bf16[512,128]{1,0:T(8,128)(2,1)}, u32[]{:S(2)}) copy-start(bf16[512,128]{1,0:T(8,128)(2,1)} %get-tuple-element.10) | copy-start | bytes 393220
  220.5 78.7 %all-to-all-start.2 = ((bf16[64,8,2560]{2,1,0:T(8,128)(2,1)}), bf16[64,8,2560]{2,1,0:T(8,128)(2,1)}, u32[]{:S(2)}, u32[]{:S(2)}) async-start(bf16[64,8,2560]{2,1,0:T(8,128)(2,1)} %fusion.2), calls=%async_computation.2 | async-start | bytes 5242880 | tf_op jit(solution)/shard_map/all_to_all | solution.py:15
  231.4 2.0 copy-start.2
  231.4 2.0 copy-start.5
  299.1 78.5 %all-to-all-start.6 = ((bf16[64,8,2560]{2,1,0:T(8,128)(2,1)}), bf16[64,8,2560]{2,1,0:T(8,128)(2,1)}, u32[]{:S(2)}, u32[]{:S(2)}) async-start(bf16[64,8,2560]{2,1,0:T(8,128)(2,1)} %fusion), calls=%async_computation.6 | async-start | bytes 5242880 | tf_op jit(solution)/shard_map/all_to_all | solution.py:15
  377.7 25.0 %all-to-all-start.3 = ((bf16[8,16,2560]{2,1,0:T(8,128)(2,1)}), bf16[8,16,2560]{2,1,0:T(8,128)(2,1)}, u32[]{:S(2)}, u32[]{:S(2)}) async-start(bf16[8,16,2560]{2,1,0:T(8,128)(2,1)} %bitcast.89), calls=%async_computation.3 | async-start | bytes 1310720 | tf_op jit(solution)/shard_map/all_to_all | solution.py:19
  402.6 22.0 %all-to-all-start.7 = ((bf16[8,16,2560]{2,1,0:T(8,128)(2,1)}), bf16[8,16,2560]{2,1,0:T(8,128)(2,1)}, u32[]{:S(2)}, u32[]{:S(2)}) async-start(bf16[8,16,2560]{2,1,0:T(8,128)(2,1)} %bitcast.88), calls=%async_computation.7 | async-start | bytes 1310720 | tf_op jit(solution)/shard_map/all_to_all | solution.py:19

commit v4 on v2

--- a/solution.py
+++ b/solution.py
@@ -1,29 +1,48 @@
 import jax
 import jax.numpy as jnp
 from jax import lax
+from jax.experimental import pallas as pl
+from jax.experimental.pallas import tpu as pltpu
 from jax.sharding import PartitionSpec as P
 
 
-def expert_rows(rows_in, cot_in, gate_weight, up_weight, down_weight):
-    gate_pre = jnp.dot(rows_in, gate_weight, preferred_element_type=jnp.float32)
-    up_pre = jnp.dot(rows_in, up_weight, preferred_element_type=jnp.float32)
-    hidden = (jax.nn.silu(gate_pre) * up_pre).astype(jnp.bfloat16)
-    partial_value = jnp.dot(hidden, down_weight, preferred_element_type=jnp.float32).astype(
+def expert_kernel(rows_ref, cot_ref, gate_ref, up_ref, down_ref, part_ref, back_ref, hid_ref, dg_ref, du_ref):
+    last_dim = (((1,), (1,)), ((), ()))
+    rows_in = rows_ref[...]
+    gate_pre = jnp.dot(rows_in, gate_ref[...], preferred_element_type=jnp.float32)
+    up_pre = jnp.dot(rows_in, up_ref[...], preferred_element_type=jnp.float32)
+    sig = 1.0 / (1.0 + jnp.exp(-gate_pre))
+    hidden = (gate_pre * sig * up_pre).astype(jnp.bfloat16)
+    hid_ref[...] = hidden
+    part_ref[...] = jnp.dot(hidden, down_ref[...], preferred_element_type=jnp.float32).astype(
         jnp.bfloat16
     )
-    first_dim = (((0,), (0,)), ((), ()))
-    last_dim = (((1,), (1,)), ((), ()))
-    grad_down = lax.dot_general(hidden, cot_in, first_dim, preferred_element_type=jnp.float32)
-    d_hidden = lax.dot_general(cot_in, down_weight, last_dim, preferred_element_type=jnp.float32)
-    sig = jax.nn.sigmoid(gate_pre)
+    d_hidden = lax.dot_general(
+        cot_ref[...], down_ref[...], last_dim, preferred_element_type=jnp.float32
+    )
     d_gate = (d_hidden * up_pre * sig * (1.0 + gate_pre * (1.0 - sig))).astype(jnp.bfloat16)
     d_up = (d_hidden * gate_pre * sig).astype(jnp.bfloat16)
+    dg_ref[...] = d_gate
+    du_ref[...] = d_up
+    back = lax.dot_general(d_gate, gate_ref[...], last_dim, preferred_element_type=jnp.float32)
+    back = back + lax.dot_general(d_up, up_ref[...], last_dim, preferred_element_type=jnp.float32)
+    back_ref[...] = back.astype(jnp.bfloat16)
+
+
+def expert_rows(rows_in, cot_in, gate_weight, up_weight, down_weight):
+    count, width = rows_in.shape
+    hidden_width = gate_weight.shape[1]
+    wide = jax.ShapeDtypeStruct((count, width), jnp.bfloat16)
+    narrow = jax.ShapeDtypeStruct((count, hidden_width), jnp.bfloat16)
+    partial_value, back_term, hidden, d_gate, d_up = pl.pallas_call(
+        expert_kernel,
+        out_shape=(wide, wide, narrow, narrow, narrow),
+        compiler_params=pltpu.CompilerParams(vmem_limit_bytes=48 * 1024 * 1024),
+    )(rows_in, cot_in, gate_weight, up_weight, down_weight)
+    first_dim = (((0,), (0,)), ((), ()))
+    grad_down = lax.dot_general(hidden, cot_in, first_dim, preferred_element_type=jnp.float32)
     grad_gate = lax.dot_general(rows_in, d_gate, first_dim, preferred_element_type=jnp.float32)
     grad_up = lax.dot_general(rows_in, d_up, first_dim, preferred_element_type=jnp.float32)
-    back_term = lax.dot_general(d_gate, gate_weight, last_dim, preferred_element_type=jnp.float32)
-    back_term = (
-        back_term + lax.dot_general(d_up, up_weight, last_dim, preferred_element_type=jnp.float32)
-    ).astype(jnp.bfloat16)
     return (partial_value, back_term, grad_gate, grad_up, grad_down)
 
 

time: 393 us -> 403 us (1.025)
  Pallas kernels: 0 us -> 11 us
  matrix products: 16.4 us -> 11.3 us
    pallas_call x0 -> x1, Pallas kernels: none -> 11 us  [expert_rows(): pl.pallas_call(expert_kernel, out_shape=(wide, wide, narrow, narrow, narr...]
    dot_general x6 -> x0, matrix products: 5.09 us -> none  [the longest x1 0.87 us: expert_rows(): up_pre = jnp.dot(rows_in, up_weight, preferred_element_type=jnp.float32)]
where the time goes in v4:
time: 403 us; the launch traced here: 397 us
  blocking collectives  332 us (82%)
  waiting for transfers between devices  20.9 us (5%)
  matrix products  11.3 us (3%)
  Pallas kernels  11 us (3%)
  starting transfers between devices  7.76 us (2%)
  local copies, waits for them, and re-layouts  7.63 us (2%)
  other arithmetic  5.96 us (1%)
    all_to_all x1, blocking collectives, body(): lax.all_to_all(send.reshape(experts, cap_hot, 2 * width), 'expert', 0, 0,...  159 us
    all_to_all x1, blocking collectives, body(): lax.all_to_all(ret.reshape(experts, cap_hot, 2 * width), 'expert', 0, 0,...  145 us
    all_to_all x1, blocking collectives, body(): lax.all_to_all(copies, 'dp', 0, 0, tiled=True)  28 us
    all_to_all x1, waiting for transfers between devices, body(): lax.all_to_all(both.reshape(dp_count, local_rows, 2 * width), 'dp', 0, 0,...  20.9 us
    pallas_call x1, Pallas kernels, expert_rows(): pl.pallas_call(expert_kernel, out_shape=(wide, wide, narrow, narrow, narr...  11 us
  transfers between devices with their start and end apart: 1, of which 1 were waited for; matrix products, arithmetic and copies ran while one was open for 2% of the time, Pallas kernels for 0%

profile of v4, /device:TPU:56, one launch (start us, length us, event | category | flops | bytes accessed | tf_op | source)
XLA Modules:
  0.0 397.3 jit_solution(11371801003221829427)
XLA Ops:
  0.6 0.7 convert_element_type.32
  1.3 0.1 copy.18
  1.4 0.7 copy.19
  2.2 1.0 concatenate.18
  3.2 0.1 broadcast_in_dim.43
  3.3 28.0 %all_to_all.20 = bf16[8,16,5248]{2,1,0:T(8,128)(2,1)S(1)} all-to-all(bf16[8,16,5248]{2,1,0:T(8,128)(2,1)S(1)} %broadcast_in_dim.43), channel_id=1, replica_groups=mesh['dp'=8,'expert'=64] {'dp'}, dimensions={0} | all-to-all | bytes 2686976 | tf_op jit(solution)/shard_map/all_to_all | solution.py:70
  31.3 0.1 eq.59
  31.4 0.1 eq.55
  31.6 0.2 slice_reduce_fusion.4
  31.8 0.6 reduce-window.6
  32.4 0.2 slice_reduce_fusion.2
  32.6 0.1 fusion.25
  32.7 0.1 reduce_sum.24
  32.9 0.2 slice_reduce_fusion.1
  33.1 0.8 convolution_convert_fusion.1
  33.9 0.8 convolution_convert_fusion
  34.7 0.8 maximum_bitcast_fusion
  35.5 158.6 %all_to_all.21 = bf16[64,8,5120]{2,1,0:T(8,128)(2,1)S(1)} all-to-all(bf16[64,8,5120]{2,1,0:T(8,128)(2,1)S(1)} %maximum_bitcast_fusion), channel_id=1, replica_groups=mesh['dp'=8,'expert'=64] {'expert'}, dimensions={0} | all-to-all | bytes 10485760 | tf_op jit(solution)/shard_map/all_to_all | solution.py:92
  194.1 0.0 copy-start.3
  194.1 0.0 copy-start
  194.1 0.0 copy-start.1
  194.1 0.0 copy-start.2
  194.1 2.7 fusion.46
  196.8 1.3 copy-done.3
  198.1 0.0 copy-done
  198.1 0.0 copy-done.1
  198.1 0.0 copy-done.2
  198.1 11.0 %shard_map.110 = (bf16[512,2560]{1,0:T(8,128)(2,1)S(1)}, bf16[512,2560]{1,0:T(8,128)(2,1)}, bf16[512,128]{1,0:T(8,128)(2,1)S(1)}, bf16[512,128]{1,0:T(8,128)(2,1)S(1)}, bf16[512,128]{1,0:T(8,128)(2,1)S(1)}) custom-call(bf16[512,2560]{1,0:T(8,128)(2,1)} %get-tuple-element.20.rows_ref, bf16[512,2560]{1,0:T(8,128)(2,1)} %get-tuple-element.19.cot_ref, ...), custom_call_target="tpu_custom_call" | custom-call | tf_op jit(solution)/shard_map/pallas_call | solution.py:37
  209.1 2.3 maximum_bitcast_fusion.1
  211.4 145.4 %all_to_all.22 = bf16[64,8,5120]{2,1,0:T(8,128)(2,1)S(1)} all-to-all(bf16[64,8,5120]{2,1,0:T(8,128)(2,1)S(1)} %maximum_bitcast_fusion.1), channel_id=1, replica_groups=mesh['dp'=8,'expert'=64] {'expert'}, dimensions={0} | all-to-all | bytes 10485760 | tf_op jit(solution)/shard_map/all_to_all | solution.py:104
  356.8 0.6 convolution_convert_fusion.6
  357.4 0.6 convolution_convert_fusion.5
  358.0 1.2 pad_maximum_fusion
  359.2 7.8 %all-to-all-start.3 = ((bf16[8,16,5120]{2,1,0:T(8,128)(2,1)}), bf16[8,16,5120]{2,1,0:T(8,128)(2,1)S(1)}, u32[]{:S(2)}, u32[]{:S(2)}) async-start(bf16[8,16,5120]{2,1,0:T(8,128)(2,1)} %pad_maximum_fusion), calls=%async_computation.3 | async-start | bytes 2621440 | tf_op jit(solution)/shard_map/all_to_all | solution.py:115
  366.9 0.0 slice-start
  366.9 3.3 fusion.2
  370.2 0.0 slice-start.1
  370.2 3.6 fusion.1
  373.8 0.0 slice-done
  373.8 0.0 slice-done.1
  373.8 1.7 fusion
  375.5 20.9 %all-to-all-done.3 = bf16[8,16,5120]{2,1,0:T(8,128)(2,1)S(1)} async-done(((bf16[8,16,5120]{2,1,0:T(8,128)(2,1)}), bf16[8,16,5120]{2,1,0:T(8,128)(2,1)S(1)}, u32[]{:S(2)}, u32[]{:S(2)}) %all-to-all-start.3) | async-done | bytes 1310752 | tf_op jit(solution)/shard_map/all_to_all | solution.py:115
  396.4 0.2 reduce_sum.25
  396.6 0.7 fusion.47
  (7 shorter events, 0.1 us)
Async XLA Ops:
  194.1 4.0 %copy-start.3 = (bf16[64,8,5120]{2,1,0:T(8,128)(2,1)}, bf16[64,8,5120]{2,1,0:T(8,128)(2,1)S(1)}, u32[]{:S(2)}) copy-start(bf16[64,8,5120]{2,1,0:T(8,128)(2,1)S(1)} %all_to_all.21) | copy-start | bytes 15728644
  194.1 4.0 %copy-start = (bf16[1,2560,128]{2,1,0:T(8,128)(2,1)S(1)}, bf16[1,2560,128]{2,1,0:T(8,128)(2,1)}, u32[]{:S(2)}) copy-start(bf16[1,2560,128]{2,1,0:T(8,128)(2,1)} %param.11) | copy-start | bytes 1966084
  194.1 4.0 %copy-start.1 = (bf16[1,2560,128]{2,1,0:T(8,128)(2,1)S(1)}, bf16[1,2560,128]{2,1,0:T(8,128)(2,1)}, u32[]{:S(2)}) copy-start(bf16[1,2560,128]{2,1,0:T(8,128)(2,1)} %param.12) | copy-start | bytes 1966084
  194.1 4.0 %copy-start.2 = (bf16[1,128,2560]{2,1,0:T(8,128)(2,1)S(1)}, bf16[1,128,2560]{2,1,0:T(8,128)(2,1)}, u32[]{:S(2)}) copy-start(bf16[1,128,2560]{2,1,0:T(8,128)(2,1)} %param.13) | copy-start | bytes 1966084
  359.2 37.2 %all-to-all-start.3 = ((bf16[8,16,5120]{2,1,0:T(8,128)(2,1)}), bf16[8,16,5120]{2,1,0:T(8,128)(2,1)S(1)}, u32[]{:S(2)}, u32[]{:S(2)}) async-start(bf16[8,16,5120]{2,1,0:T(8,128)(2,1)} %pad_maximum_fusion), calls=%async_computation.3 | async-start | bytes 2621440 | tf_op jit(solution)/shard_map/all_to_all | solution.py:115
  366.9 6.8 %slice-start = ((s8[5242880]{0:T(1024)(128)(4,1)}), s8[4194304]{0:T(1024)(128)(4,1)S(1)}, s32[]{:S(2)}) async-start(s8[5242880]{0:T(1024)(128)(4,1)} %bitcast.46), calls=%async_computation.4 | async-start | bytes 8388608
  370.2 3.6 slice-start.1

commit v5 on v2

--- a/solution.py
+++ b/solution.py
@@ -5,8 +5,11 @@
 
 
 def expert_rows(rows_in, cot_in, gate_weight, up_weight, down_weight):
-    gate_pre = jnp.dot(rows_in, gate_weight, preferred_element_type=jnp.float32)
-    up_pre = jnp.dot(rows_in, up_weight, preferred_element_type=jnp.float32)
+    hidden_width = gate_weight.shape[1]
+    both_weight = jnp.concatenate([gate_weight, up_weight], axis=1)
+    both_pre = jnp.dot(rows_in, both_weight, preferred_element_type=jnp.float32)
+    gate_pre = both_pre[:, :hidden_width]
+    up_pre = both_pre[:, hidden_width:]
     hidden = (jax.nn.silu(gate_pre) * up_pre).astype(jnp.bfloat16)
     partial_value = jnp.dot(hidden, down_weight, preferred_element_type=jnp.float32).astype(
         jnp.bfloat16
@@ -20,9 +23,9 @@
     d_up = (d_hidden * gate_pre * sig).astype(jnp.bfloat16)
     grad_gate = lax.dot_general(rows_in, d_gate, first_dim, preferred_element_type=jnp.float32)
     grad_up = lax.dot_general(rows_in, d_up, first_dim, preferred_element_type=jnp.float32)
-    back_term = lax.dot_general(d_gate, gate_weight, last_dim, preferred_element_type=jnp.float32)
-    back_term = (
-        back_term + lax.dot_general(d_up, up_weight, last_dim, preferred_element_type=jnp.float32)
+    d_both = jnp.concatenate([d_gate, d_up], axis=1)
+    back_term = lax.dot_general(
+        d_both, both_weight, last_dim, preferred_element_type=jnp.float32
     ).astype(jnp.bfloat16)
     return (partial_value, back_term, grad_gate, grad_up, grad_down)
 

time: 393 us -> 392 us (level)
  no operation moved by 1% of the time
where the time goes in v5:
time: 392 us; the launch traced here: 386 us
  blocking collectives  332 us (85%)
  waiting for transfers between devices  20.9 us (5%)
  matrix products  15 us (4%)
  starting transfers between devices  7.75 us (2%)
  local copies, waits for them, and re-layouts  5.03 us (1%)
  other arithmetic  4.49 us (1%)
    all_to_all x1, blocking collectives, body(): lax.all_to_all(send.reshape(experts, cap_hot, 2 * width), 'expert', 0, 0,...  159 us
    all_to_all x1, blocking collectives, body(): lax.all_to_all(ret.reshape(experts, cap_hot, 2 * width), 'expert', 0, 0,...  145 us
    all_to_all x1, blocking collectives, body(): lax.all_to_all(copies, 'dp', 0, 0, tiled=True)  28 us
    all_to_all x1, waiting for transfers between devices, body(): lax.all_to_all(both.reshape(dp_count, local_rows, 2 * width), 'dp', 0, 0,...  20.9 us
  transfers between devices with their start and end apart: 1, of which 1 were waited for; matrix products, arithmetic and copies ran while one was open for 2% of the time, Pallas kernels for 0%

profile of v5, /device:TPU:56, one launch (start us, length us, event | category | flops | bytes accessed | tf_op | source)
XLA Modules:
  0.0 386.1 jit_solution(3531695757256857658)
XLA Ops:
  0.6 0.0 copy-start
  0.6 0.7 convert_element_type.47
  1.4 0.1 copy.18
  1.5 0.7 copy.19
  2.2 1.0 concatenate.24
  3.3 0.1 broadcast_in_dim.43
  3.4 28.0 %all_to_all.20 = bf16[8,16,5248]{2,1,0:T(8,128)(2,1)S(1)} all-to-all(bf16[8,16,5248]{2,1,0:T(8,128)(2,1)S(1)} %broadcast_in_dim.43), channel_id=1, replica_groups=mesh['dp'=8,'expert'=64] {'dp'}, dimensions={0} | all-to-all | bytes 2686976 | tf_op jit(solution)/shard_map/all_to_all | solution.py:54
  31.3 0.2 slice_reduce_fusion.4
  31.6 0.1 eq.55
  31.7 0.1 eq.59
  31.8 0.6 reduce-window.6
  32.5 0.2 slice_reduce_fusion.2
  32.7 0.1 fusion.37
  32.8 0.1 reduce_sum.24
  33.0 0.2 slice_reduce_fusion.1
  33.1 0.8 convolution_convert_fusion.3
  34.0 0.8 convolution_convert_fusion.2
  34.8 0.8 maximum_bitcast_fusion
  35.6 0.0 copy-start.2
  35.6 0.0 copy-start.3
  35.6 158.7 %all_to_all.21 = bf16[64,8,5120]{2,1,0:T(8,128)(2,1)S(1)} all-to-all(bf16[64,8,5120]{2,1,0:T(8,128)(2,1)S(1)} %maximum_bitcast_fusion), channel_id=1, replica_groups=mesh['dp'=8,'expert'=64] {'expert'}, dimensions={0} | all-to-all | bytes 10485760 | tf_op jit(solution)/shard_map/all_to_all | solution.py:76
  194.3 0.0 copy-start.1
  194.3 0.0 copy-done.2
  194.3 0.0 copy-done.3
  194.3 0.9 fusion.10
  195.2 1.4 copy-done.1
  196.6 0.0 copy-done
  196.6 1.1 multiply_convert_fusion.1
  197.7 0.9 convolution_convert_fusion.1
  198.6 0.9 convolution_convert_fusion
  199.5 0.8 maximum_bitcast_fusion.1
  200.2 145.4 %all_to_all.22 = bf16[64,8,5120]{2,1,0:T(8,128)(2,1)S(1)} all-to-all(bf16[64,8,5120]{2,1,0:T(8,128)(2,1)S(1)} %maximum_bitcast_fusion.1), channel_id=1, replica_groups=mesh['dp'=8,'expert'=64] {'expert'}, dimensions={0} | all-to-all | bytes 10485760 | tf_op jit(solution)/shard_map/all_to_all | solution.py:88
  345.7 0.6 convolution_convert_fusion.8
  346.2 0.6 convolution_convert_fusion.7
  346.8 1.2 pad_maximum_fusion.1
  348.0 7.7 %all-to-all-start.3 = ((bf16[8,16,5120]{2,1,0:T(8,128)(2,1)}), bf16[8,16,5120]{2,1,0:T(8,128)(2,1)S(1)}, u32[]{:S(2)}, u32[]{:S(2)}) async-start(bf16[8,16,5120]{2,1,0:T(8,128)(2,1)} %pad_maximum_fusion.1), calls=%async_computation.3 | async-start | bytes 2621440 | tf_op jit(solution)/shard_map/all_to_all | solution.py:99
  355.8 0.0 slice-start
  355.8 3.2 fusion.2
  359.0 0.0 slice-start.1
  359.0 3.6 fusion
  362.6 0.0 slice-done
  362.6 0.0 slice-done.1
  362.6 1.7 fusion.1
  364.3 20.9 %all-to-all-done.3 = bf16[8,16,5120]{2,1,0:T(8,128)(2,1)S(1)} async-done(((bf16[8,16,5120]{2,1,0:T(8,128)(2,1)}), bf16[8,16,5120]{2,1,0:T(8,128)(2,1)S(1)}, u32[]{:S(2)}, u32[]{:S(2)}) %all-to-all-start.3) | async-done | bytes 1310752 | tf_op jit(solution)/shard_map/all_to_all | solution.py:99
  385.2 0.2 reduce_sum.25
  385.4 0.7 fusion.57
  (7 shorter events, 0.1 us)
Async XLA Ops:
  0.6 196.0 %copy-start = (bf16[1,128,2560]{2,1,0:T(8,128)(2,1)S(1)}, bf16[1,128,2560]{2,1,0:T(8,128)(2,1)}, u32[]{:S(2)}) copy-start(bf16[1,128,2560]{2,1,0:T(8,128)(2,1)} %param.13) | copy-start | bytes 1966084
  35.6 158.7 %copy-start.2 = (bf16[1,2560,128]{2,1,0:T(8,128)(2,1)S(1)}, bf16[1,2560,128]{2,1,0:T(8,128)(2,1)}, u32[]{:S(2)}) copy-start(bf16[1,2560,128]{2,1,0:T(8,128)(2,1)} %param.12) | copy-start | bytes 1966084
  35.6 158.7 %copy-start.3 = (bf16[1,2560,128]{2,1,0:T(8,128)(2,1)S(1)}, bf16[1,2560,128]{2,1,0:T(8,128)(2,1)}, u32[]{:S(2)}) copy-start(bf16[1,2560,128]{2,1,0:T(8,128)(2,1)} %param.11) | copy-start | bytes 1966084
  194.3 2.3 copy-start.1
  348.0 37.2 %all-to-all-start.3 = ((bf16[8,16,5120]{2,1,0:T(8,128)(2,1)}), bf16[8,16,5120]{2,1,0:T(8,128)(2,1)S(1)}, u32[]{:S(2)}, u32[]{:S(2)}) async-start(bf16[8,16,5120]{2,1,0:T(8,128)(2,1)} %pad_maximum_fusion.1), calls=%async_computation.3 | async-start | bytes 2621440 | tf_op jit(solution)/shard_map/all_to_all | solution.py:99
  355.8 6.8 %slice-start = ((s8[5242880]{0:T(1024)(128)(4,1)}), s8[4194304]{0:T(1024)(128)(4,1)S(1)}, s32[]{:S(2)}) async-start(s8[5242880]{0:T(1024)(128)(4,1)} %bitcast.56), calls=%async_computation.4 | async-start | bytes 8388608
  359.0 3.6 slice-start.1

commit v6 on v5

--- a/solution.py
+++ b/solution.py
@@ -59,8 +59,11 @@
 
     flat_ids = group_ids.reshape(-1)
     expert_range = jnp.arange(experts, dtype=jnp.int32)
-    member = (flat_ids[:, None] == expert_range[None, :]).astype(jnp.int32)
-    before = jnp.sum((jnp.cumsum(member, axis=0) - member) * member, axis=1)
+    member = (flat_ids[:, None] == expert_range[None, :]).astype(jnp.bfloat16)
+    route_range = jnp.arange(assigned, dtype=jnp.int32)
+    earlier = (route_range[None, :] < route_range[:, None]).astype(jnp.bfloat16)
+    prefix = jnp.dot(earlier, member, preferred_element_type=jnp.float32)
+    before = jnp.sum(prefix * member.astype(jnp.float32), axis=1).astype(jnp.int32)
     slot_count = experts * cap_hot
     slot_pairs = (flat_ids * cap_hot + before).astype(jnp.int32).reshape(group_rows, top_count)
     slot_range = jnp.arange(slot_count, dtype=jnp.int32)[:, None]

time: 392 us -> 391 us (level)
  no operation moved by 1% of the time
where the time goes in v6:
time: 391 us; the launch traced here: 385 us
  blocking collectives  332 us (85%)
  waiting for transfers between devices  20.9 us (5%)
  matrix products  15.2 us (4%)
  starting transfers between devices  7.76 us (2%)
  local copies, waits for them, and re-layouts  4.7 us (1%)
    all_to_all x1, blocking collectives, body(): lax.all_to_all(send.reshape(experts, cap_hot, 2 * width), 'expert', 0, 0,...  159 us
    all_to_all x1, blocking collectives, body(): lax.all_to_all(ret.reshape(experts, cap_hot, 2 * width), 'expert', 0, 0,...  145 us
    all_to_all x1, blocking collectives, body(): lax.all_to_all(copies, 'dp', 0, 0, tiled=True)  28 us
    all_to_all x1, waiting for transfers between devices, body(): lax.all_to_all(both.reshape(dp_count, local_rows, 2 * width), 'dp', 0, 0,...  20.9 us
  transfers between devices with their start and end apart: 1, of which 1 were waited for; matrix products, arithmetic and copies ran while one was open for 2% of the time, Pallas kernels for 0%

profile of v6, /device:TPU:56, one launch (start us, length us, event | category | flops | bytes accessed | tf_op | source)
XLA Modules:
  0.0 385.2 jit_solution(11514879921661839094)
XLA Ops:
  0.6 0.0 copy-start
  0.6 0.7 convert_element_type.54
  1.4 0.1 copy.17
  1.5 0.7 copy.18
  2.2 1.0 concatenate.24
  3.3 0.1 broadcast_in_dim.45
  3.4 28.0 %all_to_all.20 = bf16[8,16,5248]{2,1,0:T(8,128)(2,1)S(1)} all-to-all(bf16[8,16,5248]{2,1,0:T(8,128)(2,1)S(1)} %broadcast_in_dim.45), channel_id=1, replica_groups=mesh['dp'=8,'expert'=64] {'dp'}, dimensions={0} | all-to-all | bytes 2686976 | tf_op jit(solution)/shard_map/all_to_all | solution.py:54
  31.3 0.2 slice_reduce_fusion.3
  31.6 0.1 eq.45
  31.7 0.2 fusion.12
  31.9 0.1 convert_element_type.59
  32.1 0.2 slice_reduce_fusion.1
  32.3 0.8 convolution_convert_fusion.3
  33.1 0.8 convolution_convert_fusion.2
  33.9 0.8 maximum_bitcast_fusion
  34.7 0.0 copy-start.2
  34.7 0.0 copy-start.3
  34.7 158.7 %all_to_all.21 = bf16[64,8,5120]{2,1,0:T(8,128)(2,1)S(1)} all-to-all(bf16[64,8,5120]{2,1,0:T(8,128)(2,1)S(1)} %maximum_bitcast_fusion), channel_id=1, replica_groups=mesh['dp'=8,'expert'=64] {'expert'}, dimensions={0} | all-to-all | bytes 10485760 | tf_op jit(solution)/shard_map/all_to_all | solution.py:79
  193.4 0.0 copy-start.1
  193.4 0.0 copy-done.2
  193.4 0.0 copy-done.3
  193.4 0.9 fusion.10
  194.3 1.4 copy-done.1
  195.7 0.0 copy-done
  195.8 1.1 multiply_convert_fusion.1
  196.8 0.9 convolution_convert_fusion.1
  197.7 0.9 convolution_convert_fusion
  198.6 0.8 maximum_bitcast_fusion.1
  199.3 145.4 %all_to_all.22 = bf16[64,8,5120]{2,1,0:T(8,128)(2,1)S(1)} all-to-all(bf16[64,8,5120]{2,1,0:T(8,128)(2,1)S(1)} %maximum_bitcast_fusion.1), channel_id=1, replica_groups=mesh['dp'=8,'expert'=64] {'expert'}, dimensions={0} | all-to-all | bytes 10485760 | tf_op jit(solution)/shard_map/all_to_all | solution.py:91
  344.8 0.6 convolution_convert_fusion.8
  345.3 0.6 convolution_convert_fusion.7
  345.9 1.2 pad_maximum_fusion.1
  347.1 7.8 %all-to-all-start.3 = ((bf16[8,16,5120]{2,1,0:T(8,128)(2,1)}), bf16[8,16,5120]{2,1,0:T(8,128)(2,1)S(1)}, u32[]{:S(2)}, u32[]{:S(2)}) async-start(bf16[8,16,5120]{2,1,0:T(8,128)(2,1)} %pad_maximum_fusion.1), calls=%async_computation.3 | async-start | bytes 2621440 | tf_op jit(solution)/shard_map/all_to_all | solution.py:102
  354.9 0.0 slice-start
  354.9 3.2 fusion.2
  358.1 0.0 slice-start.1
  358.1 3.6 fusion
  361.7 0.0 slice-done
  361.7 0.0 slice-done.1
  361.7 1.7 fusion.1
  363.5 20.9 %all-to-all-done.3 = bf16[8,16,5120]{2,1,0:T(8,128)(2,1)S(1)} async-done(((bf16[8,16,5120]{2,1,0:T(8,128)(2,1)}), bf16[8,16,5120]{2,1,0:T(8,128)(2,1)S(1)}, u32[]{:S(2)}, u32[]{:S(2)}) %all-to-all-start.3) | async-done | bytes 1310752 | tf_op jit(solution)/shard_map/all_to_all | solution.py:102
  384.4 0.2 reduce_sum.22
  384.6 0.7 fusion.56
  (5 shorter events, 0.0 us)
Async XLA Ops:
  0.6 195.1 %copy-start = (bf16[1,128,2560]{2,1,0:T(8,128)(2,1)S(1)}, bf16[1,128,2560]{2,1,0:T(8,128)(2,1)}, u32[]{:S(2)}) copy-start(bf16[1,128,2560]{2,1,0:T(8,128)(2,1)} %param.13) | copy-start | bytes 1966084
  34.7 158.7 %copy-start.2 = (bf16[1,2560,128]{2,1,0:T(8,128)(2,1)S(1)}, bf16[1,2560,128]{2,1,0:T(8,128)(2,1)}, u32[]{:S(2)}) copy-start(bf16[1,2560,128]{2,1,0:T(8,128)(2,1)} %param.12) | copy-start | bytes 1966084
  34.7 158.7 %copy-start.3 = (bf16[1,2560,128]{2,1,0:T(8,128)(2,1)S(1)}, bf16[1,2560,128]{2,1,0:T(8,128)(2,1)}, u32[]{:S(2)}) copy-start(bf16[1,2560,128]{2,1,0:T(8,128)(2,1)} %param.11) | copy-start | bytes 1966084
  193.4 2.3 copy-start.1
  347.1 37.2 %all-to-all-start.3 = ((bf16[8,16,5120]{2,1,0:T(8,128)(2,1)}), bf16[8,16,5120]{2,1,0:T(8,128)(2,1)S(1)}, u32[]{:S(2)}, u32[]{:S(2)}) async-start(bf16[8,16,5120]{2,1,0:T(8,128)(2,1)} %pad_maximum_fusion.1), calls=%async_computation.3 | async-start | bytes 2621440 | tf_op jit(solution)/shard_map/all_to_all | solution.py:102
  354.9 6.8 %slice-start = ((s8[5242880]{0:T(1024)(128)(4,1)}), s8[4194304]{0:T(1024)(128)(4,1)S(1)}, s32[]{:S(2)}) async-start(s8[5242880]{0:T(1024)(128)(4,1)} %bitcast.37), calls=%async_computation.4 | async-start | bytes 8388608
  358.1 3.6 slice-start.1
